TPU v7x, 128 devices: a whole 4x4x4 slice. The times are simulated.
128 devices in a mesh: dp: 8 (over x, core), table: 16 (over z, y).
Axes of the slice: x: 4, y: 4, z: 4, core: 2. Of those that a mesh axis runs over, the one named last changes fastest.
Arguments:
- user_table: bfloat16 [524288, 256], P(('dp', 'table')), may hold values from -6 to 6
- item_table: bfloat16 [524288, 256], P(('dp', 'table')), may hold values from -6 to 6
- hist_owner: int32 [262144, 1], P(('dp', 'table')), may hold values from 0 to 127; in each aligned block of 2048 rows (0 to 2047, 2048 to 4095, ...) at most 32 rows name the same one
- hist_row: int32 [262144], P(('dp', 'table')), may hold values from 0 to 4095
- hist_seg: int32 [128, 2048], P(('dp', 'table')), may hold values from 0 to 127, never falling along the last dimension, each value on 1 to 64 neighbouring positions
- hist_wix: int32 [262144], P(('dp', 'table')), may hold values from 0 to 63
- bag_weights: bfloat16 [64], replicated, may hold values from 0.099609375 to 1
- item_owner: int32 [16384, 1], P(('dp', 'table')), may hold values from 0 to 127; in each aligned block of 128 rows (0 to 127, 128 to 255, ...) at most 2 rows name the same one
- item_row: int32 [16384], P(('dp', 'table')), may hold values from 0 to 4095
- user_proj: bfloat16 [256, 256], replicated, may hold values from -0.375 to 0.375
- item_proj: bfloat16 [256, 256], replicated, may hold values from -0.375 to 0.375
- logit_scale: float32 [1], replicated, may hold values from 8 to 600
Outputs:
- user_grad: float32 [524288, 256], P(('dp', 'table'))
- item_grad: float32 [524288, 256], P(('dp', 'table'))
- user_proj_grad: float32 [256, 256], replicated
- item_proj_grad: float32 [256, 256], replicated
Inputs may be any that keep to these rules, and one draw needn't show every extreme that they name: `hist_owner`: among the 2048 history ids of one device, no owner is named more than 32 times; some owner exactly 32 times. `item_owner`: among the 128 samples of one device, no owner is named more than 2 times; some owner exactly 2 times. `hist_seg`: each row numbers 128 samples in order; each sample has 1 to 64 ids, one has exactly 64.
All inputs are finite; a program needn't handle non-finite values.
Results may differ from a plain program's by a relative error of at most 0.01.
The roundings to bfloat16 on the way count: a program that leaves them out, or rounds other values in their place, can miss the bound.
Values may be sent and summed in bfloat16 or wider, within the bound.
No kernel may reach another device: no remote copies, remote signals or barrier semaphores. Data moves between devices by JAX's collectives and lax.ppermute only.
A program may use at most 128 MiB of HBM per device.

v0:
```python
import jax
import jax.numpy as jnp
from jax import lax
from jax.sharding import PartitionSpec as P

EPS = 1e-06
AXES = ("dp", "table")


def tower(x, weight):
    u = jnp.dot(x, weight, preferred_element_type=jnp.float32)
    r = lax.rsqrt(jnp.sum(u * u, -1, keepdims=True) + EPS)
    return (u * r, r)


def slot_rank(owner, devices):
    onehot = (owner[:, None] == jnp.arange(devices, dtype=jnp.int32)[None, :]).astype(jnp.int32)
    before = jnp.cumsum(onehot, 0) - onehot
    return jnp.sum(before * onehot, 1)


def pick_rows(table, wanted):
    rows_dev = table.shape[0]
    flat = wanted.reshape(-1)
    onehot = (flat[:, None] == jnp.arange(rows_dev, dtype=jnp.int32)[None, :]).astype(table.dtype)
    picked = jnp.dot(onehot, table, preferred_element_type=jnp.float32).astype(table.dtype)
    return picked.reshape(wanted.shape + table.shape[1:])


def add_rows(rows_dev, wanted, values):
    flat = wanted.reshape(-1)
    onehot = (jnp.arange(rows_dev, dtype=jnp.int32)[:, None] == flat[None, :]).astype(values.dtype)
    return jnp.dot(onehot, values.reshape(flat.shape[0], -1), preferred_element_type=jnp.float32)


def exchange(x):
    return lax.all_to_all(x, AXES, split_axis=1, concat_axis=1, tiled=True)


def local(
    user_table,
    item_table,
    hist_owner,
    hist_row,
    hist_seg,
    hist_wix,
    bag_weights,
    item_owner,
    item_row,
    user_proj,
    item_proj,
    logit_scale,
):
    rows_dev, width = user_table.shape
    n_dp = lax.axis_size("dp")
    n_tab = lax.axis_size("table")
    devices = n_dp * n_tab
    tokens = hist_row.shape[0]
    samples = item_row.shape[0]
    cap = max(2, 2 * tokens // devices)
    cap_item = max(2, 2 * samples // devices)
    slots = cap + cap_item
    myself = lax.axis_index(AXES)
    entries = bag_weights.shape[0]
    segment = hist_seg[0]
    sample_ids = jnp.arange(samples, dtype=jnp.int32)
    owner = jnp.concatenate([hist_owner[:, 0], item_owner[:, 0]])
    rank = jnp.concatenate(
        [slot_rank(hist_owner[:, 0], devices), cap + slot_rank(item_owner[:, 0], devices)]
    )
    row = jnp.concatenate([hist_row, item_row])
    fields = jnp.stack(
        [
            row & 255,
            row >> 8,
            jnp.concatenate([segment, sample_ids]),
            jnp.concatenate([hist_wix, jnp.zeros((samples,), jnp.int32)]),
            jnp.ones_like(row),
        ]
    )
    by_owner = (owner[None, :] == jnp.arange(devices, dtype=jnp.int32)[:, None]).astype(jnp.bfloat16)
    planes = (fields.astype(jnp.bfloat16)[:, None, :] * by_owner[None, :, :]).reshape(-1, owner.shape[0])
    by_rank = (rank[:, None] == jnp.arange(slots, dtype=jnp.int32)[None, :]).astype(jnp.bfloat16)
    table = jnp.dot(planes, by_rank, preferred_element_type=jnp.float32)
    table = table.astype(jnp.int32).reshape(fields.shape[0], devices, slots)
    table = jnp.transpose(table, (0, 2, 1)).reshape(fields.shape[0], slots * devices)
    slot_row = table[0] + 256 * table[1]
    slot_seg = table[2]
    slot_wix = table[3]
    filled = table[4] > 0
    req = jnp.where(filled, slot_row, rows_dev).reshape(slots, devices)
    is_user = jnp.arange(slots * devices, dtype=jnp.int32) < cap * devices
    want = exchange(req)
    user_want = want[:cap]
    goods_want = want[cap:]
    goods_back = exchange(pick_rows(item_table, goods_want))
    user_back = exchange(pick_rows(user_table, user_want))
    wts = jnp.sum(
        jnp.where(
            slot_wix[:, None] == jnp.arange(entries, dtype=jnp.int32)[None, :],
            bag_weights[None, :].astype(jnp.float32),
            0.0,
        ),
        1,
    ).astype(jnp.bfloat16)
    of_sample = filled[None, :] & (slot_seg[None, :] == sample_ids[:, None])
    item_pick = of_sample[:, cap * devices :].astype(jnp.bfloat16)
    item_emb = jnp.dot(
        item_pick, goods_back.reshape(-1, width), preferred_element_type=jnp.float32
    ).astype(jnp.bfloat16)
    vn, rv = tower(item_emb, item_proj)
    vh = vn.astype(jnp.bfloat16)
    vh_all = lax.all_gather(vh, AXES, axis=0, tiled=True)
    coef = jnp.where(of_sample[:, : cap * devices], wts[None, : cap * devices], jnp.zeros((), jnp.bfloat16))
    numer = jnp.dot(coef, user_back.reshape(-1, width), preferred_element_type=jnp.float32)
    denom = jnp.sum(coef.astype(jnp.float32), 1)
    bag = (numer / denom[:, None]).astype(jnp.bfloat16)
    un, ru = tower(bag, user_proj)
    uh = un.astype(jnp.bfloat16)
    uh_all = lax.all_gather(uh, AXES, axis=0, tiled=True)
    scale = logit_scale[0]
    total = vh_all.shape[0]
    mine = myself * samples + sample_ids
    everyone = jnp.arange(total, dtype=jnp.int32)
    scores = scale * jnp.dot(uh, vh_all.T, preferred_element_type=jnp.float32)
    top = jnp.max(scores, -1)
    expo = jnp.exp(scores - top[:, None])
    norm = jnp.sum(expo, -1)
    prob = expo / norm[:, None]
    hot = (everyone[None, :] == mine[:, None]).astype(jnp.float32)
    pw = (prob - hot).astype(jnp.bfloat16)
    d_un = scale / total * jnp.dot(pw, vh_all, preferred_element_type=jnp.float32)
    d_u = ru * (d_un - un * jnp.sum(un * d_un, -1, keepdims=True))
    highest = lax.Precision.HIGHEST
    user_part = jnp.dot(bag.astype(jnp.float32).T, d_u, precision=highest)
    d_bag = jnp.dot(d_u, user_proj.astype(jnp.float32).T, precision=highest)
    stats = jnp.concatenate([top, norm]).reshape(1, 1, -1)
    stats = jnp.broadcast_to(stats, (devices, 1, stats.shape[-1]))
    stats = jnp.pad(stats, ((0, 0), (0, 0), (0, -stats.shape[-1] % width)))
    stats = stats.reshape(devices, -1, width)
    user_parts = user_part.reshape(devices, -1, width)
    n_stat = stats.shape[1]
    got_s = lax.all_to_all(
        jnp.concatenate([stats, user_parts], axis=1), AXES, split_axis=0, concat_axis=0, tiled=True
    )
    flat_stats = got_s[:, :n_stat].reshape(devices, -1)
    top_all = flat_stats[:, :samples].reshape(total)
    norm_all = flat_stats[:, samples : 2 * samples].reshape(total)
    user_red = jnp.sum(got_s[:, n_stat:], 0)
    scores_c = scale * jnp.dot(vh, uh_all.T, preferred_element_type=jnp.float32)
    prob_c = jnp.exp(scores_c - top_all[None, :]) / norm_all[None, :]
    hot_c = (everyone[None, :] == mine[:, None]).astype(jnp.float32)
    pw_c = (prob_c - hot_c).astype(jnp.bfloat16)
    d_vn = scale / total * jnp.dot(pw_c, uh_all, preferred_element_type=jnp.float32)
    d_v = rv * (d_vn - vn * jnp.sum(vn * d_vn, -1, keepdims=True))
    goods_part = jnp.dot(item_emb.astype(jnp.float32).T, d_v, precision=highest)
    pick = jnp.concatenate([d_bag, d_v, denom[:, None]], axis=1)
    per_slot = jnp.dot(of_sample.T.astype(jnp.float32), pick, precision=highest)
    g_slot = (wts.astype(jnp.float32) / per_slot[:, 2 * width])[:, None] * per_slot[:, :width]
    g_slot = jnp.where(is_user[:, None], g_slot, per_slot[:, width : 2 * width])
    g_slot = jnp.where(filled[:, None], g_slot, 0.0)
    goods_parts = jnp.transpose(goods_part.reshape(devices, -1, width), (1, 0, 2))
    chunk = goods_parts.shape[0]
    hi = goods_parts.astype(jnp.bfloat16)
    lo = (goods_parts - hi.astype(jnp.float32)).astype(jnp.bfloat16)
    send = jnp.concatenate(
        [g_slot.astype(jnp.bfloat16).reshape(slots, devices, width), hi, lo], axis=0
    )
    got = exchange(send)
    tail = got[slots:].astype(jnp.float32)
    goods_red = jnp.sum(tail[:chunk] + tail[chunk:], 1)
    red = jnp.concatenate([user_red, goods_red])
    spread = lax.all_to_all(
        jnp.broadcast_to(red[None], (devices,) + red.shape), AXES, split_axis=0, concat_axis=0, tiled=True
    )
    user_proj_grad = spread[:, :chunk].reshape(width, width)
    item_proj_grad = spread[:, chunk:].reshape(width, width)
    user_grad = add_rows(rows_dev, user_want, got[:cap])
    item_grad = add_rows(rows_dev, goods_want, got[cap:slots])
    return (user_grad, item_grad, user_proj_grad, item_proj_grad)


def solution(mesh):
    in_specs = (
        P(AXES, None),
        P(AXES, None),
        P(AXES, None),
        P(AXES),
        P(AXES, None),
        P(AXES),
        P(),
        P(AXES, None),
        P(AXES),
        P(),
        P(),
        P(),
    )
    out_specs = (P(AXES, None), P(AXES, None), P(), P())
    return jax.shard_map(local, mesh=mesh, in_specs=in_specs, out_specs=out_specs, check_vma=False)
```

profile of v0, /device:TPU:1, one launch (start us, length us, event | category | flops | bytes accessed | tf_op | source)
XLA Modules:
  0.0 300.4 jit_solution(656700202510290427)
XLA Ops:
  7.3 0.9 fusion.46
  8.3 0.8 select_reduce_fusion.1
  9.2 0.8 copy.63
  10.8 0.6 fusion.30
  12.1 1.2 convolution_convert_fusion
  13.5 0.7 copy.65
  14.2 11.5 %all-to-all-start = ((s32[34,128,1]{0,2,1:T(1,128)}), s32[34,128,1]{0,2,1:T(1,128)S(1)}, u32[]{:S(2)}, u32[]{:S(2)}) async-start(s32[34,128,1]{0,2,1:T(1,128)} %copy.65), calls=%async_computation | async-start | bytes 131072 | tf_op jit(solution)/shard_map/all_to_all | solution.py:37
  25.8 9.7 %all-to-all-done = s32[34,128,1]{0,2,1:T(1,128)S(1)} async-done(((s32[34,128,1]{0,2,1:T(1,128)}), s32[34,128,1]{0,2,1:T(1,128)S(1)}, u32[]{:S(2)}, u32[]{:S(2)}) %all-to-all-start) | async-done | bytes 17440 | tf_op jit(solution)/shard_map/all_to_all | solution.py:37
  35.7 2.4 fusion.22
  38.1 0.8 copy.70
  38.9 4.3 %all-to-all-start.2 = ((bf16[2,128,256]{2,0,1:T(2,128)(2,1)}), bf16[2,128,256]{2,0,1:T(2,128)(2,1)S(1)}, u32[]{:S(2)}, u32[]{:S(2)}) async-start(bf16[2,128,256]{2,0,1:T(2,128)(2,1)} %copy.70), calls=%async_computation.2 | async-start | bytes 262144 | tf_op jit(solution)/shard_map/all_to_all | solution.py:37
  43.2 0.6 all-gather.3.cloned.1.call-start
  43.8 0.4 fusion.18
  44.1 9.3 %all-to-all-done.2 = bf16[2,128,256]{2,0,1:T(2,128)(2,1)S(1)} async-done(((bf16[2,128,256]{2,0,1:T(2,128)(2,1)}), bf16[2,128,256]{2,0,1:T(2,128)(2,1)S(1)}, u32[]{:S(2)}, u32[]{:S(2)}) %all-to-all-start.2) | async-done | bytes 131104 | tf_op jit(solution)/shard_map/all_to_all | solution.py:37
  53.9 0.7 multiply_convert_fusion
  54.7 12.3 %fusion.11 = bf16[4096,256]{1,0:T(8,128)(2,1)S(1)} fusion(bf16[4096,256]{1,0:T(8,128)(2,1)S(1)} %copy-done, s32[4096]{0:T(1024)S(1)} %bitcast.97), kind=kOutput, calls=%fused_computation.18 | convolution fusion | flops 8607760384 | bytes 4210688 | tf_op jit(solution)/shard_map/dot_general | solution.py:26
  67.0 2.5 copy.67
  69.5 4.0 %all-to-all-start.1 = ((bf16[32,128,256]{2,0,1:T(8,128)(2,1)}), bf16[32,128,256]{2,0,1:T(8,128)(2,1)S(1)}, u32[]{:S(2)}, u32[]{:S(2)}) async-start(bf16[32,128,256]{2,0,1:T(8,128)(2,1)} %copy.67), calls=%async_computation.1 | async-start | bytes 4194304 | tf_op jit(solution)/shard_map/all_to_all | solution.py:37
  74.0 0.5 convert_reduce_fusion
  74.6 30.6 %all-to-all-done.1 = bf16[32,128,256]{2,0,1:T(8,128)(2,1)S(1)} async-done(((bf16[32,128,256]{2,0,1:T(8,128)(2,1)}), bf16[32,128,256]{2,0,1:T(8,128)(2,1)S(1)}, u32[]{:S(2)}, u32[]{:S(2)}) %all-to-all-start.1) | async-done | bytes 2097184 | tf_op jit(solution)/shard_map/all_to_all | solution.py:37
  105.1 1.2 copy.68
  106.3 0.7 fusion.27
  107.3 0.7 multiply_convert_fusion.1
  108.7 22.5 %all-gather.3.cloned.1.call-done = bf16[16384,256]{1,0:T(8,128)(2,1)} async-done(((bf16[128,256]{1,0:T(8,128)(2,1)}), bf16[16384,256]{1,0:T(8,128)(2,1)}) %all-gather.3.cloned.1.call-update) | async-done | bytes 8388624 | tf_op jit(solution)/shard_map/all_gather | solution.py:113
  131.2 6.3 %fusion.56 = (f32[128]{0:T(128)S(1)}, f32[128,16384]{1,0:T(8,128)S(1)}) fusion(bf16[128,256]{1,0:T(8,128)(2,1)} %multiply_convert_fusion.1, bf16[16384,256]{1,0:T(8,128)(2,1)} %all-gather.3.cloned.1.call-done, f32[]{:T(128)} %bitcast.73), kind=kOutput, calls=%fused_computation.120 | convolution fusion | flops 1077936000 | bytes 16843268 | tf_op jit(solution)/shard_map/dot_general | solution.py:125
  137.5 1.6 fusion.10
  139.1 1.8 copy-done.2
  140.9 2.9 multiply_reduce_fusion.1
  143.8 0.4 fusion.52
  144.4 1.0 pad_maximum_fusion.1
  145.5 5.7 %all-to-all-start.3 = ((f32[128,3,256]{2,1,0:T(4,128)}), f32[128,3,256]{2,1,0:T(4,128)S(1)}, u32[]{:S(2)}, u32[]{:S(2)}) async-start(f32[128,3,256]{2,1,0:T(4,128)} %pad_maximum_fusion.1), calls=%async_computation.3 | async-start | bytes 1048576 | tf_op jit(solution)/shard_map/all_to_all | solution.py:143
  151.6 13.5 %all-to-all-done.3 = f32[128,3,256]{2,1,0:T(4,128)S(1)} async-done(((f32[128,3,256]{2,1,0:T(4,128)}), f32[128,3,256]{2,1,0:T(4,128)S(1)}, u32[]{:S(2)}, u32[]{:S(2)}) %all-to-all-start.3) | async-done | bytes 393248 | tf_op jit(solution)/shard_map/all_to_all | solution.py:143
  165.2 39.2 %all-gather.5.cloned.1.call-done = bf16[16384,256]{1,0:T(8,128)(2,1)} async-done(((bf16[128,256]{1,0:T(8,128)(2,1)}), bf16[16384,256]{1,0:T(8,128)(2,1)}) %all-gather.5.cloned.1.call-update) | async-done | bytes 8388624 | tf_op jit(solution)/shard_map/all_gather | solution.py:120
  204.4 9.9 %multiply_reduce_fusion = (f32[128]{0:T(128)S(1)}, f32[128,256]{1,0:T(8,128)S(1)}) fusion(f32[128,256]{1,0:T(8,128)S(1)} %get-tuple-element.16, f32[128]{0:T(128)S(1)} %add_rsqrt_fusion, bf16[16384,256]{1,0:T(8,128)(2,1)} %all-gather.5.cloned.1.call-done, bf16[128,256]{1,0:T(8,128)(2,1)S(1)} %copy-done.4, f32[16384]{0:T(1024)S(1)} %get-tuple-element.10, ...), kind=kOutput, calls=%fused_computation.77 | convolution fusion | flops 2162294784 | bytes 8848904 | tf_op jit(solution)/shard_map/dot_general | solution.py:154
  214.9 3.8 %fusion.37 = f32[4352,513]{0,1:T(8,128)S(1)} fusion(f32[128,1]{1,0:T(8,128)S(1)} %copy.72, f32[128,256]{1,0:T(8,128)S(1)} %subtract_multiply_fusion, f32[128,256]{1,0:T(8,128)S(1)} %fusion.53, s32[4352]{0:T(1024)S(1)} %bitcast.88, pred[4352]{0:T(1024)(128)(4,1)S(1)} %bitcast.91), kind=kOutput, calls=%fused_computation.62 | convolution fusion | flops 3430482176 | bytes 9214720 | tf_op jit(solution)/shard_map/dot_general | solution.py:158
  218.8 0.6 fusion.13
  219.4 2.4 copy.73
  221.8 1.9 pad_maximum_fusion
  223.8 2.9 copy.75
  226.7 5.7 %all-to-all-start.4 = ((bf16[38,128,256]{2,0,1:T(8,128)(2,1)}), bf16[38,128,256]{2,0,1:T(8,128)(2,1)S(1)}, u32[]{:S(2)}, u32[]{:S(2)}) async-start(bf16[38,128,256]{2,0,1:T(8,128)(2,1)} %copy.75), calls=%async_computation.4 | async-start | bytes 5242880 | tf_op jit(solution)/shard_map/all_to_all | solution.py:37
  232.7 34.3 %all-to-all-done.4 = bf16[38,128,256]{2,0,1:T(8,128)(2,1)S(1)} async-done(((bf16[38,128,256]{2,0,1:T(8,128)(2,1)}), bf16[38,128,256]{2,0,1:T(8,128)(2,1)S(1)}, u32[]{:S(2)}, u32[]{:S(2)}) %all-to-all-start.4) | async-done | bytes 2490400 | tf_op jit(solution)/shard_map/all_to_all | solution.py:37
  267.3 0.9 broadcast_in_dim.67
  268.2 5.3 %all-to-all-start.5 = ((f32[128,4,256]{2,1,0:T(4,128)}), f32[128,4,256]{2,1,0:T(4,128)S(1)}, u32[]{:S(2)}, u32[]{:S(2)}) async-start(f32[128,4,256]{2,1,0:T(4,128)} %broadcast_in_dim.67), calls=%async_computation.5 | async-start | bytes 1048576 | tf_op jit(solution)/shard_map/all_to_all | solution.py:173
  273.8 1.2 copy.80
  275.0 13.2 %fusion = f32[4096,256]{1,0:T(8,128)} fusion(bf16[4096,256]{1,0:T(8,128)(2,1)S(1)} %bitcast.78, s32[4096]{0:T(1024)S(1)} %bitcast.98), kind=kOutput, calls=%fused_computation.2 | convolution fusion | flops 8606711808 | bytes 6307840 | tf_op jit(solution)/shard_map/dot_general | solution.py:33
  288.4 2.8 fusion.17
  291.4 0.9 reshape.337
  292.3 0.9 reshape.338
  (91 shorter events, 5.9 us)
Async XLA Ops:
  7.2 47.5 %copy-start = (bf16[4096,256]{1,0:T(8,128)(2,1)S(1)}, bf16[4096,256]{1,0:T(8,128)(2,1)}, u32[]{:S(2)}) copy-start(bf16[4096,256]{1,0:T(8,128)(2,1)} %param.12) | copy-start | bytes 6291460
  7.2 3.6 %copy-start.10 = (s32[128,1]{0,1:T(1,128)S(1)}, s32[128,1]{0,1:T(1,128)}, u32[]{:S(2)}) copy-start(s32[128,1]{0,1:T(1,128)} %param.19) | copy-start | bytes 1540
  7.2 3.6 %copy-start.6 = (s32[2048,1]{0,1:T(1,128)S(1)}, s32[2048,1]{0,1:T(1,128)}, u32[]{:S(2)}) copy-start(s32[2048,1]{0,1:T(1,128)} %param.14) | copy-start | bytes 24580
  7.2 4.3 %copy-start.8 = (s32[1,2048]{1,0:T(1,128)S(1)}, s32[1,2048]{1,0:T(1,128)}, u32[]{:S(2)}) copy-start(s32[1,2048]{1,0:T(1,128)} %param.16) | copy-start | bytes 24580
  7.2 4.4 %copy-start.9 = (s32[2048]{0:T(1024)S(1)}, s32[2048]{0:T(1024)}, u32[]{:S(2)}) copy-start(s32[2048]{0:T(1024)} %param.17) | copy-start | bytes 24580
  7.2 4.5 %copy-start.7 = (s32[2048]{0:T(1024)S(1)}, s32[2048]{0:T(1024)}, u32[]{:S(2)}) copy-start(s32[2048]{0:T(1024)} %param.15) | copy-start | bytes 24580
  7.2 4.5 %copy-start.11 = (s32[128]{0:T(128)S(1)}, s32[128]{0:T(128)}, u32[]{:S(2)}) copy-start(s32[128]{0:T(128)} %param.20) | copy-start | bytes 1540
  12.1 41.5 %copy-start.5 = (bf16[256,256]{1,0:T(8,128)(2,1)S(1)}, bf16[256,256]{1,0:T(8,128)(2,1)}, u32[]{:S(2)}) copy-start(bf16[256,256]{1,0:T(8,128)(2,1)} %param.22) | copy-start | bytes 393220
  14.2 21.2 %all-to-all-start = ((s32[34,128,1]{0,2,1:T(1,128)}), s32[34,128,1]{0,2,1:T(1,128)S(1)}, u32[]{:S(2)}, u32[]{:S(2)}) async-start(s32[34,128,1]{0,2,1:T(1,128)} %copy.65), calls=%async_computation | async-start | bytes 131072 | tf_op jit(solution)/shard_map/all_to_all | solution.py:37
  38.9 14.5 %all-to-all-start.2 = ((bf16[2,128,256]{2,0,1:T(2,128)(2,1)}), bf16[2,128,256]{2,0,1:T(2,128)(2,1)S(1)}, u32[]{:S(2)}, u32[]{:S(2)}) async-start(bf16[2,128,256]{2,0,1:T(2,128)(2,1)} %copy.70), calls=%async_computation.2 | async-start | bytes 262144 | tf_op jit(solution)/shard_map/all_to_all | solution.py:37
  43.2 88.0 %all-gather.3.cloned.1.call-start = ((), (), s32[]{:S(2)}) async-start(), calls=%async_computation.6 | async-start | bytes 8454144 | tf_op jit(solution)/shard_map/all_gather | solution.py:113
  67.0 6.7 %copy-start.12 = (bf16[64]{0:T(256)(128)(2,1)S(1)}, bf16[64]{0:T(256)(128)(2,1)}, u32[]{:S(2)}) copy-start(bf16[64]{0:T(256)(128)(2,1)} %param.18) | copy-start | bytes 388
  69.5 35.6 %all-to-all-start.1 = ((bf16[32,128,256]{2,0,1:T(8,128)(2,1)}), bf16[32,128,256]{2,0,1:T(8,128)(2,1)S(1)}, u32[]{:S(2)}, u32[]{:S(2)}) async-start(bf16[32,128,256]{2,0,1:T(8,128)(2,1)} %copy.67), calls=%async_computation.1 | async-start | bytes 4194304 | tf_op jit(solution)/shard_map/all_to_all | solution.py:37
  73.5 130.9 %all-gather.5.cloned.1.call-start = ((), (), s32[]{:S(2)}) async-start(), calls=%async_computation.7 | async-start | bytes 8454144 | tf_op jit(solution)/shard_map/all_gather | solution.py:120
  74.5 32.4 %copy-start.3 = (bf16[256,256]{1,0:T(8,128)(2,1)S(1)}, bf16[256,256]{1,0:T(8,128)(2,1)}, u32[]{:S(2)}) copy-start(bf16[256,256]{1,0:T(8,128)(2,1)} %param.21) | copy-start | bytes 393220
  137.5 3.4 %copy-start.2 = (bf16[16384,256]{1,0:T(8,128)(2,1)S(1)}, bf16[16384,256]{1,0:T(8,128)(2,1)}, u32[]{:S(2)}) copy-start(bf16[16384,256]{1,0:T(8,128)(2,1)} %all-gather.3.cloned.1.call-done) | copy-start | bytes 25165828
  143.8 60.6 %copy-start.4 = (bf16[128,256]{1,0:T(8,128)(2,1)S(1)}, bf16[128,256]{1,0:T(8,128)(2,1)}, u32[]{:S(2)}) copy-start(bf16[128,256]{1,0:T(8,128)(2,1)} %multiply_convert_fusion) | copy-start | bytes 196612
  145.5 19.6 %all-to-all-start.3 = ((f32[128,3,256]{2,1,0:T(4,128)}), f32[128,3,256]{2,1,0:T(4,128)S(1)}, u32[]{:S(2)}, u32[]{:S(2)}) async-start(f32[128,3,256]{2,1,0:T(4,128)} %pad_maximum_fusion.1), calls=%async_computation.3 | async-start | bytes 1048576 | tf_op jit(solution)/shard_map/all_to_all | solution.py:143
  226.7 40.3 %all-to-all-start.4 = ((bf16[38,128,256]{2,0,1:T(8,128)(2,1)}), bf16[38,128,256]{2,0,1:T(8,128)(2,1)S(1)}, u32[]{:S(2)}, u32[]{:S(2)}) async-start(bf16[38,128,256]{2,0,1:T(8,128)(2,1)} %copy.75), calls=%async_computation.4 | async-start | bytes 5242880 | tf_op jit(solution)/shard_map/all_to_all | solution.py:37
  268.2 23.0 %all-to-all-start.5 = ((f32[128,4,256]{2,1,0:T(4,128)}), f32[128,4,256]{2,1,0:T(4,128)S(1)}, u32[]{:S(2)}, u32[]{:S(2)}) async-start(f32[128,4,256]{2,1,0:T(4,128)} %broadcast_in_dim.67), calls=%async_computation.5 | async-start | bytes 1048576 | tf_op jit(solution)/shard_map/all_to_all | solution.py:173
  288.4 4.8 %copy-start.1 = (bf16[4096,256]{1,0:T(8,128)(2,1)S(1)}, bf16[4096,256]{1,0:T(8,128)(2,1)}, u32[]{:S(2)}) copy-start(bf16[4096,256]{1,0:T(8,128)(2,1)} %param.12) | copy-start | bytes 6291460
Sparse Core Ops, SparseCore 0:
  54.8 76.3 all-gather.2
  134.9 69.4 all-gather.4
where the time goes:
time: 305 us; the launch traced here: 300 us
  waiting for transfers between devices  159 us (52%)
  matrix products  57.2 us (19%)
  starting transfers between devices  37.3 us (12%)
  local copies, waits for them, and re-layouts  19.1 us (6%)
  between operations  15.8 us (5%)
  other arithmetic  12.1 us (4%)
    all_to_all x4, waiting for transfers between devices, exchange(): return lax.all_to_all(x, AXES, split_axis=1, concat_axis=1, tiled=True)  83.8 us
    all_gather x1, waiting for transfers between devices, local(): uh_all = lax.all_gather(uh, AXES, axis=0, tiled=True)  39.2 us
    all_to_all x4, starting transfers between devices, exchange(): return lax.all_to_all(x, AXES, split_axis=1, concat_axis=1, tiled=True)  25.5 us
    all_gather x1, waiting for transfers between devices, local(): vh_all = lax.all_gather(vh, AXES, axis=0, tiled=True)  22.5 us
    dot_general x2, matrix products, add_rows(): jnp.dot(onehot, values.reshape(flat.shape[0], -1), preferred_element_type...  16 us
    dot_general x2, matrix products, pick_rows(): jnp.dot(onehot, table, preferred_element_type=jnp.float32)  14.6 us
    all_to_all x1, waiting for transfers between devices, local(): lax.all_to_all(jnp.concatenate([stats, user_parts], axis=1), AXES, split_...  13.5 us
    dot_general x1, matrix products, local(): jnp.dot(pw_c, uh_all, preferred_element_type=jnp.float32)  9.87 us
  transfers between devices with their start and end apart: 8, of which 7 were waited for; matrix products, arithmetic and copies ran while one was open for 17% of the time, Pallas kernels for 0%

commit v1 on v0

--- a/solution.py
+++ b/solution.py
@@ -134,6 +134,13 @@
     highest = lax.Precision.HIGHEST
     user_part = jnp.dot(bag.astype(jnp.float32).T, d_u, precision=highest)
     d_bag = jnp.dot(d_u, user_proj.astype(jnp.float32).T, precision=highest)
+    n_user = cap * devices
+    pick = jnp.concatenate([d_bag, denom[:, None]], axis=1)
+    per_slot = jnp.dot(of_sample[:, :n_user].T.astype(jnp.float32), pick, precision=highest)
+    g_slot = (wts[:n_user].astype(jnp.float32) / per_slot[:, width])[:, None] * per_slot[:, :width]
+    g_slot = jnp.where(filled[:n_user, None], g_slot, 0.0)
+    got_user = exchange(g_slot.astype(jnp.bfloat16).reshape(cap, devices, width))
+    user_grad = add_rows(rows_dev, user_want, got_user)
     stats = jnp.concatenate([top, norm]).reshape(1, 1, -1)
     stats = jnp.broadcast_to(stats, (devices, 1, stats.shape[-1]))
     stats = jnp.pad(stats, ((0, 0), (0, 0), (0, -stats.shape[-1] % width)))
@@ -154,20 +161,16 @@
     d_vn = scale / total * jnp.dot(pw_c, uh_all, preferred_element_type=jnp.float32)
     d_v = rv * (d_vn - vn * jnp.sum(vn * d_vn, -1, keepdims=True))
     goods_part = jnp.dot(item_emb.astype(jnp.float32).T, d_v, precision=highest)
-    pick = jnp.concatenate([d_bag, d_v, denom[:, None]], axis=1)
-    per_slot = jnp.dot(of_sample.T.astype(jnp.float32), pick, precision=highest)
-    g_slot = (wts.astype(jnp.float32) / per_slot[:, 2 * width])[:, None] * per_slot[:, :width]
-    g_slot = jnp.where(is_user[:, None], g_slot, per_slot[:, width : 2 * width])
-    g_slot = jnp.where(filled[:, None], g_slot, 0.0)
+    d_v_slot = jnp.dot(item_pick.T.astype(jnp.float32), d_v, precision=highest)
     goods_parts = jnp.transpose(goods_part.reshape(devices, -1, width), (1, 0, 2))
     chunk = goods_parts.shape[0]
     hi = goods_parts.astype(jnp.bfloat16)
     lo = (goods_parts - hi.astype(jnp.float32)).astype(jnp.bfloat16)
     send = jnp.concatenate(
-        [g_slot.astype(jnp.bfloat16).reshape(slots, devices, width), hi, lo], axis=0
+        [d_v_slot.astype(jnp.bfloat16).reshape(cap_item, devices, width), hi, lo], axis=0
     )
     got = exchange(send)
-    tail = got[slots:].astype(jnp.float32)
+    tail = got[cap_item:].astype(jnp.float32)
     goods_red = jnp.sum(tail[:chunk] + tail[chunk:], 1)
     red = jnp.concatenate([user_red, goods_red])
     spread = lax.all_to_all(
@@ -175,8 +178,7 @@
     )
     user_proj_grad = spread[:, :chunk].reshape(width, width)
     item_proj_grad = spread[:, chunk:].reshape(width, width)
-    user_grad = add_rows(rows_dev, user_want, got[:cap])
-    item_grad = add_rows(rows_dev, goods_want, got[cap:slots])
+    item_grad = add_rows(rows_dev, goods_want, got[:cap_item])
     return (user_grad, item_grad, user_proj_grad, item_proj_grad)
 
 

time: 305 us -> 289 us (0.948)
  waiting for transfers between devices: 159 us -> 130 us
  other arithmetic: 12.1 us -> 18 us
  local copies, waits for them, and re-layouts: 19.1 us -> 22.4 us
    all_to_all x4 -> x5, waiting for transfers between devices: 83.8 us -> 59.9 us  [exchange(): return lax.all_to_all(x, AXES, split_axis=1, concat_axis=1, tiled=True)]
    all_to_all x1, waiting for transfers between devices: 13.5 us -> 7.28 us  [local(): lax.all_to_all(jnp.concatenate([stats, user_parts], axis=1), AXES, split_...]
    all_to_all x4 -> x5, starting transfers between devices: 25.5 us -> 29.8 us  [exchange(): return lax.all_to_all(x, AXES, split_axis=1, concat_axis=1, tiled=True)]
    reshape x0 -> x2, local copies, waits for them, and re-layouts: none -> 3.58 us  [the longest x1 3.45 us: local(): g_slot.astype(jnp.bfloat16).reshape(cap, devices, width)]
  transfers between devices with their start and end apart: 8 -> 9, of which waited for: 7 -> 7; matrix products, arithmetic and copies ran while one was open for 17% -> 26% of each run, Pallas kernels for 0% -> 0%
where the time goes in v1:
time: 289 us; the launch traced here: 284 us
  waiting for transfers between devices  130 us (45%)
  matrix products  57.4 us (20%)
  starting transfers between devices  40.3 us (14%)
  local copies, waits for them, and re-layouts  22.4 us (8%)
  other arithmetic  18 us (6%)
  between operations  15.5 us (5%)
    all_to_all x5, waiting for transfers between devices, exchange(): return lax.all_to_all(x, AXES, split_axis=1, concat_axis=1, tiled=True)  59.9 us
    all_gather x1, waiting for transfers between devices, local(): uh_all = lax.all_gather(uh, AXES, axis=0, tiled=True)  40.6 us
    all_to_all x5, starting transfers between devices, exchange(): return lax.all_to_all(x, AXES, split_axis=1, concat_axis=1, tiled=True)  29.8 us
    all_gather x1, waiting for transfers between devices, local(): vh_all = lax.all_gather(vh, AXES, axis=0, tiled=True)  22.3 us
    dot_general x2, matrix products, add_rows(): jnp.dot(onehot, values.reshape(flat.shape[0], -1), preferred_element_type...  17.7 us
    dot_general x2, matrix products, pick_rows(): jnp.dot(onehot, table, preferred_element_type=jnp.float32)  14.7 us
    dot_general x1, matrix products, local(): jnp.dot(pw_c, uh_all, preferred_element_type=jnp.float32)  9.92 us
    all_to_all x1, waiting for transfers between devices, local(): lax.all_to_all(jnp.concatenate([stats, user_parts], axis=1), AXES, split_...  7.28 us
  transfers between devices with their start and end apart: 9, of which 7 were waited for; matrix products, arithmetic and copies ran while one was open for 26% of the time, Pallas kernels for 0%

profile of v1, /device:TPU:1, one launch (start us, length us, event | category | flops | bytes accessed | tf_op | source)
XLA Modules:
  0.0 283.7 jit_solution(8847906912940397657)
XLA Ops:
  7.2 0.9 fusion.47
  8.1 0.7 pad_add_fusion
  8.9 0.7 convert_reduce_fusion.1
  10.6 0.8 select_reduce_fusion.1
  11.4 0.8 copy.59
  12.6 1.0 copy-done.4
  13.6 1.3 broadcast_add_fusion
  16.3 1.2 convolution_convert_fusion.1
  17.7 0.7 copy.61
  18.5 11.5 %all-to-all-start = ((s32[34,128,1]{0,2,1:T(1,128)}), s32[34,128,1]{0,2,1:T(1,128)S(1)}, u32[]{:S(2)}, u32[]{:S(2)}) async-start(s32[34,128,1]{0,2,1:T(1,128)} %copy.61), calls=%async_computation | async-start | bytes 131072 | tf_op jit(solution)/shard_map/all_to_all | solution.py:37
  30.0 9.7 %all-to-all-done = s32[34,128,1]{0,2,1:T(1,128)S(1)} async-done(((s32[34,128,1]{0,2,1:T(1,128)}), s32[34,128,1]{0,2,1:T(1,128)S(1)}, u32[]{:S(2)}, u32[]{:S(2)}) %all-to-all-start) | async-done | bytes 17440 | tf_op jit(solution)/shard_map/all_to_all | solution.py:37
  39.9 2.4 fusion.25
  42.3 0.8 copy.66
  43.1 4.3 %all-to-all-start.2 = ((bf16[2,128,256]{2,0,1:T(2,128)(2,1)}), bf16[2,128,256]{2,0,1:T(2,128)(2,1)S(1)}, u32[]{:S(2)}, u32[]{:S(2)}) async-start(bf16[2,128,256]{2,0,1:T(2,128)(2,1)} %copy.66), calls=%async_computation.2 | async-start | bytes 262144 | tf_op jit(solution)/shard_map/all_to_all | solution.py:37
  48.4 9.3 %all-to-all-done.2 = bf16[2,128,256]{2,0,1:T(2,128)(2,1)S(1)} async-done(((bf16[2,128,256]{2,0,1:T(2,128)(2,1)}), bf16[2,128,256]{2,0,1:T(2,128)(2,1)S(1)}, u32[]{:S(2)}, u32[]{:S(2)}) %all-to-all-start.2) | async-done | bytes 131104 | tf_op jit(solution)/shard_map/all_to_all | solution.py:37
  58.1 0.7 multiply_convert_fusion
  58.9 12.3 %fusion.11 = bf16[4096,256]{1,0:T(8,128)(2,1)S(1)} fusion(bf16[4096,256]{1,0:T(8,128)(2,1)S(1)} %copy-done, s32[4096]{0:T(1024)S(1)} %bitcast.98), kind=kOutput, calls=%fused_computation.18 | convolution fusion | flops 8607760384 | bytes 4210688 | tf_op jit(solution)/shard_map/dot_general | solution.py:26
  71.2 2.5 copy.63
  73.7 4.0 %all-to-all-start.1 = ((bf16[32,128,256]{2,0,1:T(8,128)(2,1)}), bf16[32,128,256]{2,0,1:T(8,128)(2,1)S(1)}, u32[]{:S(2)}, u32[]{:S(2)}) async-start(bf16[32,128,256]{2,0,1:T(8,128)(2,1)} %copy.63), calls=%async_computation.1 | async-start | bytes 4194304 | tf_op jit(solution)/shard_map/all_to_all | solution.py:37
  78.8 30.6 %all-to-all-done.1 = bf16[32,128,256]{2,0,1:T(8,128)(2,1)S(1)} async-done(((bf16[32,128,256]{2,0,1:T(8,128)(2,1)}), bf16[32,128,256]{2,0,1:T(8,128)(2,1)S(1)}, u32[]{:S(2)}, u32[]{:S(2)}) %all-to-all-start.1) | async-done | bytes 2097184 | tf_op jit(solution)/shard_map/all_to_all | solution.py:37
  109.4 1.2 copy.64
  111.5 0.7 multiply_convert_fusion.1
  113.1 22.3 %all-gather.3.cloned.1.call-done = bf16[16384,256]{1,0:T(8,128)(2,1)} async-done(((bf16[128,256]{1,0:T(8,128)(2,1)}), bf16[16384,256]{1,0:T(8,128)(2,1)}) %all-gather.3.cloned.1.call-update) | async-done | bytes 8388624 | tf_op jit(solution)/shard_map/all_gather | solution.py:113
  135.4 6.3 %fusion.57 = (f32[128]{0:T(128)S(1)}, f32[128,16384]{1,0:T(8,128)S(1)}) fusion(bf16[128,256]{1,0:T(8,128)(2,1)} %multiply_convert_fusion.1, bf16[16384,256]{1,0:T(8,128)(2,1)} %all-gather.3.cloned.1.call-done, f32[]{:T(128)} %bitcast.77), kind=kOutput, calls=%fused_computation.122 | convolution fusion | flops 1077936000 | bytes 16843268 | tf_op jit(solution)/shard_map/dot_general | solution.py:125
  141.7 1.6 fusion.10
  143.3 1.8 copy-done.3
  145.1 2.9 %multiply_reduce_fusion.1 = (f32[128]{0:T(128)S(1)}, f32[128,256]{1,0:T(8,128)S(1)}) fusion(f32[128,256]{1,0:T(8,128)S(1)} %get-tuple-element.21, f32[128]{0:T(128)S(1)} %add_rsqrt_fusion.1, bf16[16384,256]{1,0:T(8,128)(2,1)S(1)} %copy-done.3, f32[128,16384]{1,0:T(8,128)S(1)} %get-tuple-element.23, s32[128]{0:T(128)S(1)} %iota_add_fusion, ...), kind=kOutput, calls=%fused_computation.79 | convolution fusion | flops 1086455680 | bytes 17041924 | tf_op jit(solution)/shard_map/dot_general | solution.py:132
  148.3 2.0 fusion.23
  150.3 2.0 copy-done.2
  152.9 1.0 pad_maximum_fusion
  154.0 5.4 %all-to-all-start.4 = ((f32[128,3,256]{2,1,0:T(4,128)}), f32[128,3,256]{2,1,0:T(4,128)S(1)}, u32[]{:S(2)}, u32[]{:S(2)}) async-start(f32[128,3,256]{2,1,0:T(4,128)} %pad_maximum_fusion), calls=%async_computation.4 | async-start | bytes 1048576 | tf_op jit(solution)/shard_map/all_to_all | solution.py:150
  159.4 2.8 fusion.19
  162.7 3.4 %copy.69 = bf16[32,128,256]{2,0,1:T(8,128)(2,1)} copy(bf16[32,128,256]{1,0,2:T(8,128)(2,1)S(1)} %bitcast.80) | data formatting | bytes 4194304 | tf_op jit(solution)/shard_map/reshape | solution.py:142
  166.1 7.3 %all-to-all-done.4 = f32[128,3,256]{2,1,0:T(4,128)S(1)} async-done(((f32[128,3,256]{2,1,0:T(4,128)}), f32[128,3,256]{2,1,0:T(4,128)S(1)}, u32[]{:S(2)}, u32[]{:S(2)}) %all-to-all-start.4) | async-done | bytes 393248 | tf_op jit(solution)/shard_map/all_to_all | solution.py:150
  173.4 4.0 %all-to-all-start.3 = ((bf16[32,128,256]{2,0,1:T(8,128)(2,1)}), bf16[32,128,256]{2,0,1:T(8,128)(2,1)S(1)}, u32[]{:S(2)}, u32[]{:S(2)}) async-start(bf16[32,128,256]{2,0,1:T(8,128)(2,1)} %copy.69), calls=%async_computation.3 | async-start | bytes 4194304 | tf_op jit(solution)/shard_map/all_to_all | solution.py:37
  178.2 40.6 %all-gather.5.cloned.1.call-done = bf16[16384,256]{1,0:T(8,128)(2,1)} async-done(((bf16[128,256]{1,0:T(8,128)(2,1)}), bf16[16384,256]{1,0:T(8,128)(2,1)}) %all-gather.5.cloned.1.call-update) | async-done | bytes 8388624 | tf_op jit(solution)/shard_map/all_gather | solution.py:120
  218.8 9.9 %multiply_reduce_fusion = (f32[128]{0:T(128)S(1)}, f32[128,256]{1,0:T(8,128)S(1)}) fusion(f32[128,256]{1,0:T(8,128)S(1)} %get-tuple-element.19, f32[128]{0:T(128)S(1)} %add_rsqrt_fusion, bf16[16384,256]{1,0:T(8,128)(2,1)} %all-gather.5.cloned.1.call-done, bf16[128,256]{1,0:T(8,128)(2,1)} %multiply_convert_fusion, f32[16384]{0:T(1024)} %get-tuple-element.15, ...), kind=kOutput, calls=%fused_computation.77 | convolution fusion | flops 2162294784 | bytes 8848904 | tf_op jit(solution)/shard_map/dot_general | solution.py:161
  229.9 1.2 pad_maximum_fusion.1
  231.2 6.0 %all-to-all-start.5 = ((bf16[6,128,256]{2,0,1:T(8,128)(2,1)}), bf16[6,128,256]{2,0,1:T(8,128)(2,1)S(1)}, u32[]{:S(2)}, u32[]{:S(2)}) async-start(bf16[6,128,256]{2,0,1:T(8,128)(2,1)} %pad_maximum_fusion.1), calls=%async_computation.5 | async-start | bytes 1048576 | tf_op jit(solution)/shard_map/all_to_all | solution.py:37
  237.2 1.2 slice_reduce_fusion
  238.4 2.5 copy.70
  240.9 10.3 %all-to-all-done.5 = bf16[6,128,256]{2,0,1:T(8,128)(2,1)S(1)} async-done(((bf16[6,128,256]{2,0,1:T(8,128)(2,1)}), bf16[6,128,256]{2,0,1:T(8,128)(2,1)S(1)}, u32[]{:S(2)}, u32[]{:S(2)}) %all-to-all-start.5) | async-done | bytes 393248 | tf_op jit(solution)/shard_map/all_to_all | solution.py:37
  251.6 0.9 broadcast_in_dim.55
  252.5 4.4 %all-to-all-start.6 = ((f32[128,4,256]{2,1,0:T(4,128)}), f32[128,4,256]{2,1,0:T(4,128)S(1)}, u32[]{:S(2)}, u32[]{:S(2)}) async-start(f32[128,4,256]{2,1,0:T(4,128)} %broadcast_in_dim.55), calls=%async_computation.6 | async-start | bytes 1048576 | tf_op jit(solution)/shard_map/all_to_all | solution.py:176
  256.8 14.9 %fusion = f32[4096,256]{1,0:T(8,128)} fusion(bf16[4096,256]{1,0:T(8,128)(2,1)} %bitcast.81, s32[4096]{0:T(1024)S(1)} %bitcast.99), kind=kOutput, calls=%fused_computation.2 | convolution fusion | flops 8606711808 | bytes 6307840 | tf_op jit(solution)/shard_map/dot_general | solution.py:33
  271.8 2.8 fusion.17
  274.8 0.9 reshape.322
  275.7 0.9 reshape.323
  (90 shorter events, 10.8 us)
Async XLA Ops:
  7.2 51.8 %copy-start = (bf16[4096,256]{1,0:T(8,128)(2,1)S(1)}, bf16[4096,256]{1,0:T(8,128)(2,1)}, u32[]{:S(2)}) copy-start(bf16[4096,256]{1,0:T(8,128)(2,1)} %param.12) | copy-start | bytes 6291460
  7.2 8.0 %copy-start.8 = (s32[2048,1]{0,1:T(1,128)S(1)}, s32[2048,1]{0,1:T(1,128)}, u32[]{:S(2)}) copy-start(s32[2048,1]{0,1:T(1,128)} %param.14) | copy-start | bytes 24580
  7.2 8.7 %copy-start.10 = (s32[128]{0:T(128)S(1)}, s32[128]{0:T(128)}, u32[]{:S(2)}) copy-start(s32[128]{0:T(128)} %param.20) | copy-start | bytes 1540
  7.2 8.7 %copy-start.9 = (s32[2048]{0:T(1024)S(1)}, s32[2048]{0:T(1024)}, u32[]{:S(2)}) copy-start(s32[2048]{0:T(1024)} %param.15) | copy-start | bytes 24580
  12.6 1.0 copy-start.4
  16.3 41.5 %copy-start.7 = (bf16[256,256]{1,0:T(8,128)(2,1)S(1)}, bf16[256,256]{1,0:T(8,128)(2,1)}, u32[]{:S(2)}) copy-start(bf16[256,256]{1,0:T(8,128)(2,1)} %param.22) | copy-start | bytes 393220
  18.5 21.2 %all-to-all-start = ((s32[34,128,1]{0,2,1:T(1,128)}), s32[34,128,1]{0,2,1:T(1,128)S(1)}, u32[]{:S(2)}, u32[]{:S(2)}) async-start(s32[34,128,1]{0,2,1:T(1,128)} %copy.61), calls=%async_computation | async-start | bytes 131072 | tf_op jit(solution)/shard_map/all_to_all | solution.py:37
  43.1 14.5 %all-to-all-start.2 = ((bf16[2,128,256]{2,0,1:T(2,128)(2,1)}), bf16[2,128,256]{2,0,1:T(2,128)(2,1)S(1)}, u32[]{:S(2)}, u32[]{:S(2)}) async-start(bf16[2,128,256]{2,0,1:T(2,128)(2,1)} %copy.66), calls=%async_computation.2 | async-start | bytes 262144 | tf_op jit(solution)/shard_map/all_to_all | solution.py:37
  47.4 88.0 %all-gather.3.cloned.1.call-start = ((), (), s32[]{:S(2)}) async-start(), calls=%async_computation.7 | async-start | bytes 8454144 | tf_op jit(solution)/shard_map/all_gather | solution.py:113
  71.2 6.7 %copy-start.11 = (bf16[64]{0:T(256)(128)(2,1)S(1)}, bf16[64]{0:T(256)(128)(2,1)}, u32[]{:S(2)}) copy-start(bf16[64]{0:T(256)(128)(2,1)} %param.18) | copy-start | bytes 388
  73.7 35.6 %all-to-all-start.1 = ((bf16[32,128,256]{2,0,1:T(8,128)(2,1)}), bf16[32,128,256]{2,0,1:T(8,128)(2,1)S(1)}, u32[]{:S(2)}, u32[]{:S(2)}) async-start(bf16[32,128,256]{2,0,1:T(8,128)(2,1)} %copy.63), calls=%async_computation.1 | async-start | bytes 4194304 | tf_op jit(solution)/shard_map/all_to_all | solution.py:37
  77.7 141.1 %all-gather.5.cloned.1.call-start = ((), (), s32[]{:S(2)}) async-start(), calls=%async_computation.8 | async-start | bytes 8454144 | tf_op jit(solution)/shard_map/all_gather | solution.py:120
  78.8 32.4 %copy-start.6 = (bf16[256,256]{1,0:T(8,128)(2,1)S(1)}, bf16[256,256]{1,0:T(8,128)(2,1)}, u32[]{:S(2)}) copy-start(bf16[256,256]{1,0:T(8,128)(2,1)} %param.21) | copy-start | bytes 393220
  141.7 3.4 %copy-start.3 = (bf16[16384,256]{1,0:T(8,128)(2,1)S(1)}, bf16[16384,256]{1,0:T(8,128)(2,1)}, u32[]{:S(2)}) copy-start(bf16[16384,256]{1,0:T(8,128)(2,1)} %all-gather.3.cloned.1.call-done) | copy-start | bytes 25165828
  150.3 2.0 copy-start.2
  154.0 19.4 %all-to-all-start.4 = ((f32[128,3,256]{2,1,0:T(4,128)}), f32[128,3,256]{2,1,0:T(4,128)S(1)}, u32[]{:S(2)}, u32[]{:S(2)}) async-start(f32[128,3,256]{2,1,0:T(4,128)} %pad_maximum_fusion), calls=%async_computation.4 | async-start | bytes 1048576 | tf_op jit(solution)/shard_map/all_to_all | solution.py:150
  173.4 55.3 %copy-start.5 = (f32[128,3,256]{2,1,0:T(4,128)}, f32[128,3,256]{2,1,0:T(4,128)S(1)}, u32[]{:S(2)}) copy-start(f32[128,3,256]{2,1,0:T(4,128)S(1)} %all-to-all-done.4) | copy-start | bytes 1179652
  173.4 57.7 %all-to-all-start.3 = ((bf16[32,128,256]{2,0,1:T(8,128)(2,1)}), bf16[32,128,256]{2,0,1:T(8,128)(2,1)S(1)}, u32[]{:S(2)}, u32[]{:S(2)}) async-start(bf16[32,128,256]{2,0,1:T(8,128)(2,1)} %copy.69), calls=%async_computation.3 | async-start | bytes 4194304 | tf_op jit(solution)/shard_map/all_to_all | solution.py:37
  231.2 20.1 %all-to-all-start.5 = ((bf16[6,128,256]{2,0,1:T(8,128)(2,1)}), bf16[6,128,256]{2,0,1:T(8,128)(2,1)S(1)}, u32[]{:S(2)}, u32[]{:S(2)}) async-start(bf16[6,128,256]{2,0,1:T(8,128)(2,1)} %pad_maximum_fusion.1), calls=%async_computation.5 | async-start | bytes 1048576 | tf_op jit(solution)/shard_map/all_to_all | solution.py:37
  252.5 22.2 %all-to-all-start.6 = ((f32[128,4,256]{2,1,0:T(4,128)}), f32[128,4,256]{2,1,0:T(4,128)S(1)}, u32[]{:S(2)}, u32[]{:S(2)}) async-start(f32[128,4,256]{2,1,0:T(4,128)} %broadcast_in_dim.55), calls=%async_computation.6 | async-start | bytes 1048576 | tf_op jit(solution)/shard_map/all_to_all | solution.py:176
  271.8 4.8 %copy-start.1 = (bf16[4096,256]{1,0:T(8,128)(2,1)S(1)}, bf16[4096,256]{1,0:T(8,128)(2,1)}, u32[]{:S(2)}) copy-start(bf16[4096,256]{1,0:T(8,128)(2,1)} %param.12) | copy-start | bytes 6291460
Sparse Core Ops, SparseCore 0:
  59.0 76.3 all-gather.2
  139.1 79.6 all-gather.4

commit v2 on v1

--- a/solution.py
+++ b/solution.py
@@ -145,7 +145,7 @@
     stats = jnp.broadcast_to(stats, (devices, 1, stats.shape[-1]))
     stats = jnp.pad(stats, ((0, 0), (0, 0), (0, -stats.shape[-1] % width)))
     stats = stats.reshape(devices, -1, width)
-    user_parts = user_part.reshape(devices, -1, width)
+    user_parts = jnp.transpose(user_part.reshape(-1, devices, width), (1, 0, 2))
     n_stat = stats.shape[1]
     got_s = lax.all_to_all(
         jnp.concatenate([stats, user_parts], axis=1), AXES, split_axis=0, concat_axis=0, tiled=True
@@ -155,14 +155,14 @@
     norm_all = flat_stats[:, samples : 2 * samples].reshape(total)
     user_red = jnp.sum(got_s[:, n_stat:], 0)
     scores_c = scale * jnp.dot(vh, uh_all.T, preferred_element_type=jnp.float32)
-    prob_c = jnp.exp(scores_c - top_all[None, :]) / norm_all[None, :]
+    prob_c = jnp.exp(scores_c - top_all[None, :]) * (1.0 / norm_all)[None, :]
     hot_c = (everyone[None, :] == mine[:, None]).astype(jnp.float32)
     pw_c = (prob_c - hot_c).astype(jnp.bfloat16)
     d_vn = scale / total * jnp.dot(pw_c, uh_all, preferred_element_type=jnp.float32)
     d_v = rv * (d_vn - vn * jnp.sum(vn * d_vn, -1, keepdims=True))
     goods_part = jnp.dot(item_emb.astype(jnp.float32).T, d_v, precision=highest)
     d_v_slot = jnp.dot(item_pick.T.astype(jnp.float32), d_v, precision=highest)
-    goods_parts = jnp.transpose(goods_part.reshape(devices, -1, width), (1, 0, 2))
+    goods_parts = goods_part.reshape(-1, devices, width)
     chunk = goods_parts.shape[0]
     hi = goods_parts.astype(jnp.bfloat16)
     lo = (goods_parts - hi.astype(jnp.float32)).astype(jnp.bfloat16)
@@ -173,11 +173,9 @@
     tail = got[cap_item:].astype(jnp.float32)
     goods_red = jnp.sum(tail[:chunk] + tail[chunk:], 1)
     red = jnp.concatenate([user_red, goods_red])
-    spread = lax.all_to_all(
-        jnp.broadcast_to(red[None], (devices,) + red.shape), AXES, split_axis=0, concat_axis=0, tiled=True
-    )
-    user_proj_grad = spread[:, :chunk].reshape(width, width)
-    item_proj_grad = spread[:, chunk:].reshape(width, width)
+    spread = exchange(jnp.broadcast_to(red[:, None], (red.shape[0], devices, width)))
+    user_proj_grad = spread[:chunk].reshape(width, width)
+    item_proj_grad = spread[chunk:].reshape(width, width)
     item_grad = add_rows(rows_dev, goods_want, got[:cap_item])
     return (user_grad, item_grad, user_proj_grad, item_proj_grad)
 

time: 289 us -> 289 us (level)
    all_to_all x1 -> x0, starting transfers between devices: 4.37 us -> none  [local(): lax.all_to_all(jnp.broadcast_to(red[None], (devices,) + red.shape), AXES,...]
    all_to_all x5 -> x6, starting transfers between devices: 29.8 us -> 34.2 us  [exchange(): return lax.all_to_all(x, AXES, split_axis=1, concat_axis=1, tiled=True)]
    unnamed x28 -> x30, local copies, waits for them, and re-layouts: 5.39 us -> 6.83 us
    all_to_all x5 -> x6, waiting for transfers between devices: 59.9 us -> 59.9 us  [exchange(): return lax.all_to_all(x, AXES, split_axis=1, concat_axis=1, tiled=True)]
  transfers between devices with their start and end apart: 9 -> 9, of which waited for: 7 -> 7; matrix products, arithmetic and copies ran while one was open for 26% -> 27% of each run, Pallas kernels for 0% -> 0%
where the time goes in v2:
time: 289 us; the launch traced here: 284 us
  waiting for transfers between devices  130 us (45%)
  matrix products  57.4 us (20%)
  starting transfers between devices  40.3 us (14%)
  local copies, waits for them, and re-layouts  21.6 us (7%)
  other arithmetic  18.7 us (6%)
  between operations  15.5 us (5%)
    all_to_all x6, waiting for transfers between devices, exchange(): return lax.all_to_all(x, AXES, split_axis=1, concat_axis=1, tiled=True)  59.9 us
    all_gather x1, waiting for transfers between devices, local(): uh_all = lax.all_gather(uh, AXES, axis=0, tiled=True)  40.6 us
    all_to_all x6, starting transfers between devices, exchange(): return lax.all_to_all(x, AXES, split_axis=1, concat_axis=1, tiled=True)  34.2 us
    all_gather x1, waiting for transfers between devices, local(): vh_all = lax.all_gather(vh, AXES, axis=0, tiled=True)  22.3 us
    dot_general x2, matrix products, add_rows(): jnp.dot(onehot, values.reshape(flat.shape[0], -1), preferred_element_type...  17.7 us
    dot_general x2, matrix products, pick_rows(): jnp.dot(onehot, table, preferred_element_type=jnp.float32)  14.7 us
    dot_general x1, matrix products, local(): jnp.dot(pw_c, uh_all, preferred_element_type=jnp.float32)  9.92 us
    all_to_all x1, waiting for transfers between devices, local(): lax.all_to_all(jnp.concatenate([stats, user_parts], axis=1), AXES, split_...  7.28 us
  transfers between devices with their start and end apart: 9, of which 7 were waited for; matrix products, arithmetic and copies ran while one was open for 27% of the time, Pallas kernels for 0%

profile of v2, /device:TPU:1, one launch (start us, length us, event | category | flops | bytes accessed | tf_op | source)
XLA Modules:
  0.0 283.6 jit_solution(170055418482812964)
XLA Ops:
  7.2 0.9 fusion.47
  8.1 0.7 pad_add_fusion
  8.9 0.7 convert_reduce_fusion.1
  10.6 0.8 select_reduce_fusion.1
  11.4 0.8 copy.70
  12.6 1.0 copy-done.4
  13.6 1.3 broadcast_add_fusion
  16.3 1.2 convolution_convert_fusion.1
  17.7 0.7 copy.72
  18.5 11.5 %all-to-all-start = ((s32[34,128,1]{0,2,1:T(1,128)}), s32[34,128,1]{0,2,1:T(1,128)S(1)}, u32[]{:S(2)}, u32[]{:S(2)}) async-start(s32[34,128,1]{0,2,1:T(1,128)} %copy.72), calls=%async_computation | async-start | bytes 131072 | tf_op jit(solution)/shard_map/all_to_all | solution.py:37
  30.0 9.7 %all-to-all-done = s32[34,128,1]{0,2,1:T(1,128)S(1)} async-done(((s32[34,128,1]{0,2,1:T(1,128)}), s32[34,128,1]{0,2,1:T(1,128)S(1)}, u32[]{:S(2)}, u32[]{:S(2)}) %all-to-all-start) | async-done | bytes 17440 | tf_op jit(solution)/shard_map/all_to_all | solution.py:37
  39.9 2.4 fusion.25
  42.3 0.8 copy.77
  43.1 4.3 %all-to-all-start.2 = ((bf16[2,128,256]{2,0,1:T(2,128)(2,1)}), bf16[2,128,256]{2,0,1:T(2,128)(2,1)S(1)}, u32[]{:S(2)}, u32[]{:S(2)}) async-start(bf16[2,128,256]{2,0,1:T(2,128)(2,1)} %copy.77), calls=%async_computation.2 | async-start | bytes 262144 | tf_op jit(solution)/shard_map/all_to_all | solution.py:37
  48.4 9.3 %all-to-all-done.2 = bf16[2,128,256]{2,0,1:T(2,128)(2,1)S(1)} async-done(((bf16[2,128,256]{2,0,1:T(2,128)(2,1)}), bf16[2,128,256]{2,0,1:T(2,128)(2,1)S(1)}, u32[]{:S(2)}, u32[]{:S(2)}) %all-to-all-start.2) | async-done | bytes 131104 | tf_op jit(solution)/shard_map/all_to_all | solution.py:37
  58.1 0.7 multiply_convert_fusion
  58.9 12.3 %fusion.11 = bf16[4096,256]{1,0:T(8,128)(2,1)S(1)} fusion(bf16[4096,256]{1,0:T(8,128)(2,1)S(1)} %copy-done, s32[4096]{0:T(1024)S(1)} %bitcast.105), kind=kOutput, calls=%fused_computation.18 | convolution fusion | flops 8607760384 | bytes 4210688 | tf_op jit(solution)/shard_map/dot_general | solution.py:26
  71.2 2.5 copy.74
  73.7 4.0 %all-to-all-start.1 = ((bf16[32,128,256]{2,0,1:T(8,128)(2,1)}), bf16[32,128,256]{2,0,1:T(8,128)(2,1)S(1)}, u32[]{:S(2)}, u32[]{:S(2)}) async-start(bf16[32,128,256]{2,0,1:T(8,128)(2,1)} %copy.74), calls=%async_computation.1 | async-start | bytes 4194304 | tf_op jit(solution)/shard_map/all_to_all | solution.py:37
  78.8 30.6 %all-to-all-done.1 = bf16[32,128,256]{2,0,1:T(8,128)(2,1)S(1)} async-done(((bf16[32,128,256]{2,0,1:T(8,128)(2,1)}), bf16[32,128,256]{2,0,1:T(8,128)(2,1)S(1)}, u32[]{:S(2)}, u32[]{:S(2)}) %all-to-all-start.1) | async-done | bytes 2097184 | tf_op jit(solution)/shard_map/all_to_all | solution.py:37
  109.4 1.2 copy.75
  111.5 0.7 multiply_convert_fusion.1
  113.1 22.3 %all-gather.3.cloned.1.call-done = bf16[16384,256]{1,0:T(8,128)(2,1)} async-done(((bf16[128,256]{1,0:T(8,128)(2,1)}), bf16[16384,256]{1,0:T(8,128)(2,1)}) %all-gather.3.cloned.1.call-update) | async-done | bytes 8388624 | tf_op jit(solution)/shard_map/all_gather | solution.py:113
  135.4 6.3 %fusion.57 = (f32[128]{0:T(128)S(1)}, f32[128,16384]{1,0:T(8,128)S(1)}) fusion(bf16[128,256]{1,0:T(8,128)(2,1)} %multiply_convert_fusion.1, bf16[16384,256]{1,0:T(8,128)(2,1)} %all-gather.3.cloned.1.call-done, f32[]{:T(128)} %bitcast.78), kind=kOutput, calls=%fused_computation.123 | convolution fusion | flops 1077936000 | bytes 16843268 | tf_op jit(solution)/shard_map/dot_general | solution.py:125
  141.7 1.6 fusion.10
  143.3 1.8 copy-done.3
  145.1 2.9 %multiply_reduce_fusion.1 = (f32[128]{0:T(128)S(1)}, f32[128,256]{1,0:T(8,128)S(1)}) fusion(f32[128,256]{1,0:T(8,128)S(1)} %get-tuple-element.19, f32[128]{0:T(128)S(1)} %add_rsqrt_fusion.1, bf16[16384,256]{1,0:T(8,128)(2,1)S(1)} %copy-done.3, f32[128,16384]{1,0:T(8,128)S(1)} %get-tuple-element.21, s32[128]{0:T(128)S(1)} %iota_add_fusion, ...), kind=kOutput, calls=%fused_computation.79 | convolution fusion | flops 1086455680 | bytes 17041924 | tf_op jit(solution)/shard_map/dot_general | solution.py:132
  148.3 2.0 fusion.22
  150.3 2.0 copy-done.2
  153.0 1.0 pad_maximum_fusion
  154.0 5.4 %all-to-all-start.4 = ((f32[128,3,256]{2,1,0:T(4,128)}), f32[128,3,256]{2,1,0:T(4,128)S(1)}, u32[]{:S(2)}, u32[]{:S(2)}) async-start(f32[128,3,256]{2,1,0:T(4,128)} %pad_maximum_fusion), calls=%async_computation.4 | async-start | bytes 1048576 | tf_op jit(solution)/shard_map/all_to_all | solution.py:150
  159.4 2.8 fusion.19
  162.7 3.4 %copy.80 = bf16[32,128,256]{2,0,1:T(8,128)(2,1)} copy(bf16[32,128,256]{1,0,2:T(8,128)(2,1)S(1)} %bitcast.81) | data formatting | bytes 4194304 | tf_op jit(solution)/shard_map/reshape | solution.py:142
  166.2 7.3 %all-to-all-done.4 = f32[128,3,256]{2,1,0:T(4,128)S(1)} async-done(((f32[128,3,256]{2,1,0:T(4,128)}), f32[128,3,256]{2,1,0:T(4,128)S(1)}, u32[]{:S(2)}, u32[]{:S(2)}) %all-to-all-start.4) | async-done | bytes 393248 | tf_op jit(solution)/shard_map/all_to_all | solution.py:150
  173.5 4.0 %all-to-all-start.3 = ((bf16[32,128,256]{2,0,1:T(8,128)(2,1)}), bf16[32,128,256]{2,0,1:T(8,128)(2,1)S(1)}, u32[]{:S(2)}, u32[]{:S(2)}) async-start(bf16[32,128,256]{2,0,1:T(8,128)(2,1)} %copy.80), calls=%async_computation.3 | async-start | bytes 4194304 | tf_op jit(solution)/shard_map/all_to_all | solution.py:37
  178.3 40.6 %all-gather.5.cloned.1.call-done = bf16[16384,256]{1,0:T(8,128)(2,1)} async-done(((bf16[128,256]{1,0:T(8,128)(2,1)}), bf16[16384,256]{1,0:T(8,128)(2,1)}) %all-gather.5.cloned.1.call-update) | async-done | bytes 8388624 | tf_op jit(solution)/shard_map/all_gather | solution.py:120
  218.9 9.9 %multiply_reduce_fusion = (f32[128]{0:T(128)S(1)}, f32[128,256]{1,0:T(8,128)S(1)}) fusion(f32[128,256]{1,0:T(8,128)S(1)} %get-tuple-element.17, f32[128]{0:T(128)S(1)} %add_rsqrt_fusion, bf16[16384,256]{1,0:T(8,128)(2,1)} %all-gather.5.cloned.1.call-done, bf16[128,256]{1,0:T(8,128)(2,1)} %multiply_convert_fusion, f32[16384]{0:T(1024)} %get-tuple-element.13, ...), kind=kOutput, calls=%fused_computation.77 | convolution fusion | flops 2162294784 | bytes 8848904 | tf_op jit(solution)/shard_map/dot_general | solution.py:161
  230.1 1.2 pad_maximum_fusion.1
  231.3 6.0 %all-to-all-start.5 = ((bf16[6,128,256]{2,0,1:T(8,128)(2,1)}), bf16[6,128,256]{2,0,1:T(8,128)(2,1)S(1)}, u32[]{:S(2)}, u32[]{:S(2)}) async-start(bf16[6,128,256]{2,0,1:T(8,128)(2,1)} %pad_maximum_fusion.1), calls=%async_computation.5 | async-start | bytes 1048576 | tf_op jit(solution)/shard_map/all_to_all | solution.py:37
  237.4 1.2 slice_reduce_fusion
  238.6 2.5 copy.81
  241.1 10.3 %all-to-all-done.5 = bf16[6,128,256]{2,0,1:T(8,128)(2,1)S(1)} async-done(((bf16[6,128,256]{2,0,1:T(8,128)(2,1)}), bf16[6,128,256]{2,0,1:T(8,128)(2,1)S(1)}, u32[]{:S(2)}, u32[]{:S(2)}) %all-to-all-start.5) | async-done | bytes 393248 | tf_op jit(solution)/shard_map/all_to_all | solution.py:37
  251.8 0.9 broadcast_in_dim.55
  252.7 4.4 %all-to-all-start.6 = ((f32[4,128,256]{2,0,1:T(4,128)}), f32[4,128,256]{2,0,1:T(4,128)S(1)}, u32[]{:S(2)}, u32[]{:S(2)}) async-start(f32[4,128,256]{2,0,1:T(4,128)} %broadcast_in_dim.55), calls=%async_computation.6 | async-start | bytes 1048576 | tf_op jit(solution)/shard_map/all_to_all | solution.py:37
  257.0 14.9 %fusion = f32[4096,256]{1,0:T(8,128)} fusion(bf16[4096,256]{1,0:T(8,128)(2,1)} %bitcast.84, s32[4096]{0:T(1024)S(1)} %bitcast.106), kind=kOutput, calls=%fused_computation.2 | convolution fusion | flops 8606711808 | bytes 6307840 | tf_op jit(solution)/shard_map/dot_general | solution.py:33
  272.0 2.8 fusion.17
  275.0 0.7 copy.92
  275.8 0.7 copy.93
  (90 shorter events, 11.0 us)
Async XLA Ops:
  7.2 51.8 %copy-start = (bf16[4096,256]{1,0:T(8,128)(2,1)S(1)}, bf16[4096,256]{1,0:T(8,128)(2,1)}, u32[]{:S(2)}) copy-start(bf16[4096,256]{1,0:T(8,128)(2,1)} %param.12) | copy-start | bytes 6291460
  7.2 8.0 %copy-start.8 = (s32[2048,1]{0,1:T(1,128)S(1)}, s32[2048,1]{0,1:T(1,128)}, u32[]{:S(2)}) copy-start(s32[2048,1]{0,1:T(1,128)} %param.14) | copy-start | bytes 24580
  7.2 8.7 %copy-start.10 = (s32[128]{0:T(128)S(1)}, s32[128]{0:T(128)}, u32[]{:S(2)}) copy-start(s32[128]{0:T(128)} %param.20) | copy-start | bytes 1540
  7.2 8.7 %copy-start.9 = (s32[2048]{0:T(1024)S(1)}, s32[2048]{0:T(1024)}, u32[]{:S(2)}) copy-start(s32[2048]{0:T(1024)} %param.15) | copy-start | bytes 24580
  12.6 1.0 copy-start.4
  16.3 41.5 %copy-start.7 = (bf16[256,256]{1,0:T(8,128)(2,1)S(1)}, bf16[256,256]{1,0:T(8,128)(2,1)}, u32[]{:S(2)}) copy-start(bf16[256,256]{1,0:T(8,128)(2,1)} %param.22) | copy-start | bytes 393220
  18.5 21.2 %all-to-all-start = ((s32[34,128,1]{0,2,1:T(1,128)}), s32[34,128,1]{0,2,1:T(1,128)S(1)}, u32[]{:S(2)}, u32[]{:S(2)}) async-start(s32[34,128,1]{0,2,1:T(1,128)} %copy.72), calls=%async_computation | async-start | bytes 131072 | tf_op jit(solution)/shard_map/all_to_all | solution.py:37
  43.1 14.5 %all-to-all-start.2 = ((bf16[2,128,256]{2,0,1:T(2,128)(2,1)}), bf16[2,128,256]{2,0,1:T(2,128)(2,1)S(1)}, u32[]{:S(2)}, u32[]{:S(2)}) async-start(bf16[2,128,256]{2,0,1:T(2,128)(2,1)} %copy.77), calls=%async_computation.2 | async-start | bytes 262144 | tf_op jit(solution)/shard_map/all_to_all | solution.py:37
  47.4 88.0 %all-gather.3.cloned.1.call-start = ((), (), s32[]{:S(2)}) async-start(), calls=%async_computation.7 | async-start | bytes 8454144 | tf_op jit(solution)/shard_map/all_gather | solution.py:113
  71.2 6.7 %copy-start.11 = (bf16[64]{0:T(256)(128)(2,1)S(1)}, bf16[64]{0:T(256)(128)(2,1)}, u32[]{:S(2)}) copy-start(bf16[64]{0:T(256)(128)(2,1)} %param.18) | copy-start | bytes 388
  73.7 35.6 %all-to-all-start.1 = ((bf16[32,128,256]{2,0,1:T(8,128)(2,1)}), bf16[32,128,256]{2,0,1:T(8,128)(2,1)S(1)}, u32[]{:S(2)}, u32[]{:S(2)}) async-start(bf16[32,128,256]{2,0,1:T(8,128)(2,1)} %copy.74), calls=%async_computation.1 | async-start | bytes 4194304 | tf_op jit(solution)/shard_map/all_to_all | solution.py:37
  77.7 141.1 %all-gather.5.cloned.1.call-start = ((), (), s32[]{:S(2)}) async-start(), calls=%async_computation.8 | async-start | bytes 8454144 | tf_op jit(solution)/shard_map/all_gather | solution.py:120
  78.8 32.4 %copy-start.6 = (bf16[256,256]{1,0:T(8,128)(2,1)S(1)}, bf16[256,256]{1,0:T(8,128)(2,1)}, u32[]{:S(2)}) copy-start(bf16[256,256]{1,0:T(8,128)(2,1)} %param.21) | copy-start | bytes 393220
  141.7 3.4 %copy-start.3 = (bf16[16384,256]{1,0:T(8,128)(2,1)S(1)}, bf16[16384,256]{1,0:T(8,128)(2,1)}, u32[]{:S(2)}) copy-start(bf16[16384,256]{1,0:T(8,128)(2,1)} %all-gather.3.cloned.1.call-done) | copy-start | bytes 25165828
  150.3 2.0 copy-start.2
  154.0 19.4 %all-to-all-start.4 = ((f32[128,3,256]{2,1,0:T(4,128)}), f32[128,3,256]{2,1,0:T(4,128)S(1)}, u32[]{:S(2)}, u32[]{:S(2)}) async-start(f32[128,3,256]{2,1,0:T(4,128)} %pad_maximum_fusion), calls=%async_computation.4 | async-start | bytes 1048576 | tf_op jit(solution)/shard_map/all_to_all | solution.py:150
  173.5 55.3 %copy-start.5 = (f32[128,3,256]{2,1,0:T(4,128)}, f32[128,3,256]{2,1,0:T(4,128)S(1)}, u32[]{:S(2)}) copy-start(f32[128,3,256]{2,1,0:T(4,128)S(1)} %all-to-all-done.4) | copy-start | bytes 1179652
  173.5 57.9 %all-to-all-start.3 = ((bf16[32,128,256]{2,0,1:T(8,128)(2,1)}), bf16[32,128,256]{2,0,1:T(8,128)(2,1)S(1)}, u32[]{:S(2)}, u32[]{:S(2)}) async-start(bf16[32,128,256]{2,0,1:T(8,128)(2,1)} %copy.80), calls=%async_computation.3 | async-start | bytes 4194304 | tf_op jit(solution)/shard_map/all_to_all | solution.py:37
  231.3 20.1 %all-to-all-start.5 = ((bf16[6,128,256]{2,0,1:T(8,128)(2,1)}), bf16[6,128,256]{2,0,1:T(8,128)(2,1)S(1)}, u32[]{:S(2)}, u32[]{:S(2)}) async-start(bf16[6,128,256]{2,0,1:T(8,128)(2,1)} %pad_maximum_fusion.1), calls=%async_computation.5 | async-start | bytes 1048576 | tf_op jit(solution)/shard_map/all_to_all | solution.py:37
  252.7 22.2 %all-to-all-start.6 = ((f32[4,128,256]{2,0,1:T(4,128)}), f32[4,128,256]{2,0,1:T(4,128)S(1)}, u32[]{:S(2)}, u32[]{:S(2)}) async-start(f32[4,128,256]{2,0,1:T(4,128)} %broadcast_in_dim.55), calls=%async_computation.6 | async-start | bytes 1048576 | tf_op jit(solution)/shard_map/all_to_all | solution.py:37
  272.0 4.5 %copy-start.1 = (bf16[4096,256]{1,0:T(8,128)(2,1)S(1)}, bf16[4096,256]{1,0:T(8,128)(2,1)}, u32[]{:S(2)}) copy-start(bf16[4096,256]{1,0:T(8,128)(2,1)} %param.12) | copy-start | bytes 6291460
Sparse Core Ops, SparseCore 0:
  59.0 76.3 all-gather.2
  139.1 79.7 all-gather.4

commit v3 on v1

--- a/solution.py
+++ b/solution.py
@@ -2,6 +2,8 @@
 import jax.numpy as jnp
 from jax import lax
 from jax.sharding import PartitionSpec as P
+from jax.experimental import pallas as pl
+from jax.experimental.pallas import tpu as pltpu
 
 EPS = 1e-06
 AXES = ("dp", "table")
@@ -35,6 +37,53 @@
 
 def exchange(x):
     return lax.all_to_all(x, AXES, split_axis=1, concat_axis=1, tiled=True)
+
+
+def _column_kernel(base_ref, scale_ref, vh_ref, uh_ref, top_ref, norm_ref, out_ref, acc_ref):
+    b = pl.program_id(0)
+    rows, block = vh_ref.shape[0], uh_ref.shape[0]
+
+    @pl.when(b == 0)
+    def _():
+        acc_ref[...] = jnp.zeros_like(acc_ref)
+
+    uh = uh_ref[...]
+    s = scale_ref[0] * lax.dot_general(
+        vh_ref[...], uh, (((1,), (1,)), ((), ())), preferred_element_type=jnp.float32
+    )
+    p = jnp.exp(s - top_ref[...]) / norm_ref[...]
+    col = b * block + lax.broadcasted_iota(jnp.int32, (rows, block), 1)
+    mine = base_ref[0] + lax.broadcasted_iota(jnp.int32, (rows, block), 0)
+    pw = (p - (col == mine).astype(jnp.float32)).astype(jnp.bfloat16)
+    acc_ref[...] += jnp.dot(pw, uh, preferred_element_type=jnp.float32)
+
+    @pl.when(b == pl.num_programs(0) - 1)
+    def _():
+        out_ref[...] = acc_ref[...]
+
+
+def column_side(base, scale, vh, uh_all, top_all, norm_all, block=2048):
+    rows, width = vh.shape
+    total = uh_all.shape[0]
+    grid_spec = pltpu.PrefetchScalarGridSpec(
+        num_scalar_prefetch=1,
+        grid=(total // block,),
+        in_specs=[
+            pl.BlockSpec(memory_space=pltpu.SMEM),
+            pl.BlockSpec((rows, width), lambda b, base: (0, 0)),
+            pl.BlockSpec((block, width), lambda b, base: (b, 0)),
+            pl.BlockSpec((1, block), lambda b, base: (0, b)),
+            pl.BlockSpec((1, block), lambda b, base: (0, b)),
+        ],
+        out_specs=pl.BlockSpec((rows, width), lambda b, base: (0, 0)),
+        scratch_shapes=[pltpu.VMEM((rows, width), jnp.float32)],
+    )
+    return pl.pallas_call(
+        _column_kernel,
+        out_shape=jax.ShapeDtypeStruct((rows, width), jnp.float32),
+        grid_spec=grid_spec,
+        compiler_params=pltpu.CompilerParams(dimension_semantics=("arbitrary",)),
+    )(base.reshape(1), scale.reshape(1), vh, uh_all, top_all[None], norm_all[None])
 
 
 def local(
@@ -154,11 +203,7 @@
     top_all = flat_stats[:, :samples].reshape(total)
     norm_all = flat_stats[:, samples : 2 * samples].reshape(total)
     user_red = jnp.sum(got_s[:, n_stat:], 0)
-    scores_c = scale * jnp.dot(vh, uh_all.T, preferred_element_type=jnp.float32)
-    prob_c = jnp.exp(scores_c - top_all[None, :]) / norm_all[None, :]
-    hot_c = (everyone[None, :] == mine[:, None]).astype(jnp.float32)
-    pw_c = (prob_c - hot_c).astype(jnp.bfloat16)
-    d_vn = scale / total * jnp.dot(pw_c, uh_all, preferred_element_type=jnp.float32)
+    d_vn = scale / total * column_side(myself * samples, scale, vh, uh_all, top_all, norm_all)
     d_v = rv * (d_vn - vn * jnp.sum(vn * d_vn, -1, keepdims=True))
     goods_part = jnp.dot(item_emb.astype(jnp.float32).T, d_v, precision=highest)
     d_v_slot = jnp.dot(item_pick.T.astype(jnp.float32), d_v, precision=highest)

time: 289 us -> 292 us (1.010)
  Pallas kernels: 0 us -> 9.88 us
  matrix products: 57.4 us -> 49.3 us
    dot_general x1 -> x0, matrix products: 9.92 us -> none  [local(): jnp.dot(pw_c, uh_all, preferred_element_type=jnp.float32)]
    pallas_call x0 -> x1, Pallas kernels: none -> 9.88 us  [column_side(): pl.pallas_call(_column_kernel, out_shape=jax.ShapeDtypeStruct((rows, widt...]
  transfers between devices with their start and end apart: 9 -> 9, of which waited for: 7 -> 7; matrix products, arithmetic and copies ran while one was open for 26% -> 24% of each run, Pallas kernels for 0% -> 3%
where the time goes in v3:
time: 292 us; the launch traced here: 287 us
  waiting for transfers between devices  130 us (45%)
  matrix products  49.3 us (17%)
  starting transfers between devices  40.3 us (14%)
  local copies, waits for them, and re-layouts  22.4 us (8%)
  other arithmetic  19 us (7%)
  between operations  15.5 us (5%)
  Pallas kernels  9.88 us (3%)
    all_to_all x5, waiting for transfers between devices, exchange(): return lax.all_to_all(x, AXES, split_axis=1, concat_axis=1, tiled=True)  59.9 us
    all_gather x1, waiting for transfers between devices, local(): uh_all = lax.all_gather(uh, AXES, axis=0, tiled=True)  40.6 us
    all_to_all x5, starting transfers between devices, exchange(): return lax.all_to_all(x, AXES, split_axis=1, concat_axis=1, tiled=True)  29.8 us
    all_gather x1, waiting for transfers between devices, local(): vh_all = lax.all_gather(vh, AXES, axis=0, tiled=True)  22.3 us
    dot_general x2, matrix products, add_rows(): jnp.dot(onehot, values.reshape(flat.shape[0], -1), preferred_element_type...  17.7 us
    dot_general x2, matrix products, pick_rows(): jnp.dot(onehot, table, preferred_element_type=jnp.float32)  14.7 us
    pallas_call x1, Pallas kernels, column_side(): pl.pallas_call(_column_kernel, out_shape=jax.ShapeDtypeStruct((rows, widt...  9.88 us
    all_to_all x1, waiting for transfers between devices, local(): lax.all_to_all(jnp.concatenate([stats, user_parts], axis=1), AXES, split_...  7.29 us
  transfers between devices with their start and end apart: 9, of which 7 were waited for; matrix products, arithmetic and copies ran while one was open for 24% of the time, Pallas kernels for 3%

profile of v3, /device:TPU:1, one launch (start us, length us, event | category | flops | bytes accessed | tf_op | source)
XLA Modules:
  0.0 286.6 jit_solution(11473868706598982803)
XLA Ops:
  7.2 0.9 fusion.36
  10.6 0.8 select_reduce_fusion.1
  11.4 0.8 copy.61
  12.6 1.0 copy-done.4
  13.6 1.3 broadcast_add_fusion
  16.3 1.2 convolution_convert_fusion.1
  17.7 0.7 copy.63
  18.5 11.5 %all-to-all-start = ((s32[34,128,1]{0,2,1:T(1,128)}), s32[34,128,1]{0,2,1:T(1,128)S(1)}, u32[]{:S(2)}, u32[]{:S(2)}) async-start(s32[34,128,1]{0,2,1:T(1,128)} %copy.63), calls=%async_computation | async-start | bytes 131072 | tf_op jit(solution)/shard_map/all_to_all | solution.py:39
  30.0 9.7 %all-to-all-done = s32[34,128,1]{0,2,1:T(1,128)S(1)} async-done(((s32[34,128,1]{0,2,1:T(1,128)}), s32[34,128,1]{0,2,1:T(1,128)S(1)}, u32[]{:S(2)}, u32[]{:S(2)}) %all-to-all-start) | async-done | bytes 17440 | tf_op jit(solution)/shard_map/all_to_all | solution.py:39
  39.9 2.4 fusion.17
  42.3 0.8 copy.68
  43.1 4.3 %all-to-all-start.2 = ((bf16[2,128,256]{2,0,1:T(2,128)(2,1)}), bf16[2,128,256]{2,0,1:T(2,128)(2,1)S(1)}, u32[]{:S(2)}, u32[]{:S(2)}) async-start(bf16[2,128,256]{2,0,1:T(2,128)(2,1)} %copy.68), calls=%async_computation.2 | async-start | bytes 262144 | tf_op jit(solution)/shard_map/all_to_all | solution.py:39
  48.4 9.3 %all-to-all-done.2 = bf16[2,128,256]{2,0,1:T(2,128)(2,1)S(1)} async-done(((bf16[2,128,256]{2,0,1:T(2,128)(2,1)}), bf16[2,128,256]{2,0,1:T(2,128)(2,1)S(1)}, u32[]{:S(2)}, u32[]{:S(2)}) %all-to-all-start.2) | async-done | bytes 131104 | tf_op jit(solution)/shard_map/all_to_all | solution.py:39
  58.1 0.7 multiply_convert_fusion.vh_ref
  58.9 12.3 %fusion.5 = bf16[4096,256]{1,0:T(8,128)(2,1)S(1)} fusion(bf16[4096,256]{1,0:T(8,128)(2,1)S(1)} %copy-done, s32[4096]{0:T(1024)S(1)} %bitcast.95), kind=kOutput, calls=%fused_computation.11 | convolution fusion | flops 8607760384 | bytes 4210688 | tf_op jit(solution)/shard_map/dot_general | solution.py:28
  71.2 2.5 copy.65
  73.7 4.0 %all-to-all-start.1 = ((bf16[32,128,256]{2,0,1:T(8,128)(2,1)}), bf16[32,128,256]{2,0,1:T(8,128)(2,1)S(1)}, u32[]{:S(2)}, u32[]{:S(2)}) async-start(bf16[32,128,256]{2,0,1:T(8,128)(2,1)} %copy.65), calls=%async_computation.1 | async-start | bytes 4194304 | tf_op jit(solution)/shard_map/all_to_all | solution.py:39
  78.8 30.6 %all-to-all-done.1 = bf16[32,128,256]{2,0,1:T(8,128)(2,1)S(1)} async-done(((bf16[32,128,256]{2,0,1:T(8,128)(2,1)}), bf16[32,128,256]{2,0,1:T(8,128)(2,1)S(1)}, u32[]{:S(2)}, u32[]{:S(2)}) %all-to-all-start.1) | async-done | bytes 2097184 | tf_op jit(solution)/shard_map/all_to_all | solution.py:39
  109.4 1.2 copy.66
  113.1 22.3 %all-gather.3.cloned.1.call-done = bf16[16384,256]{1,0:T(8,128)(2,1)} async-done(((bf16[128,256]{1,0:T(8,128)(2,1)}), bf16[16384,256]{1,0:T(8,128)(2,1)}) %all-gather.3.cloned.1.call-update) | async-done | bytes 8388624 | tf_op jit(solution)/shard_map/all_gather | solution.py:162
  135.4 6.3 %fusion.47 = (f32[128]{0:T(128)S(1)}, f32[128,16384]{1,0:T(8,128)S(1)}) fusion(bf16[128,256]{1,0:T(8,128)(2,1)} %multiply_convert_fusion.1, bf16[16384,256]{1,0:T(8,128)(2,1)} %all-gather.3.cloned.1.call-done, f32[]{:T(128)} %bitcast.73), kind=kOutput, calls=%fused_computation.112 | convolution fusion | flops 1077936000 | bytes 16843268 | tf_op jit(solution)/shard_map/dot_general | solution.py:174
  141.7 1.6 fusion.4
  143.3 1.8 copy-done.3
  145.1 2.9 %multiply_reduce_fusion.1 = (f32[128]{0:T(128)S(1)}, f32[128,256]{1,0:T(8,128)S(1)}) fusion(f32[128,256]{1,0:T(8,128)S(1)} %get-tuple-element.21, f32[128]{0:T(128)S(1)} %add_rsqrt_fusion.1, bf16[16384,256]{1,0:T(8,128)(2,1)S(1)} %copy-done.3, f32[128,16384]{1,0:T(8,128)S(1)} %get-tuple-element.23, s32[128]{0:T(128)S(1)} %iota_add_fusion, ...), kind=kOutput, calls=%fused_computation.70 | convolution fusion | flops 1086455680 | bytes 17041924 | tf_op jit(solution)/shard_map/dot_general | solution.py:181
  148.3 2.0 fusion.15
  150.3 2.0 copy-done.2
  152.9 1.0 pad_maximum_fusion
  154.0 5.4 %all-to-all-start.4 = ((f32[128,3,256]{2,1,0:T(4,128)}), f32[128,3,256]{2,1,0:T(4,128)S(1)}, u32[]{:S(2)}, u32[]{:S(2)}) async-start(f32[128,3,256]{2,1,0:T(4,128)} %pad_maximum_fusion), calls=%async_computation.4 | async-start | bytes 1048576 | tf_op jit(solution)/shard_map/all_to_all | solution.py:199
  159.4 2.8 fusion.12
  162.7 3.4 %copy.71 = bf16[32,128,256]{2,0,1:T(8,128)(2,1)} copy(bf16[32,128,256]{1,0,2:T(8,128)(2,1)S(1)} %bitcast.75) | data formatting | bytes 4194304 | tf_op jit(solution)/shard_map/reshape | solution.py:191
  166.1 7.3 %all-to-all-done.4 = f32[128,3,256]{2,1,0:T(4,128)S(1)} async-done(((f32[128,3,256]{2,1,0:T(4,128)}), f32[128,3,256]{2,1,0:T(4,128)S(1)}, u32[]{:S(2)}, u32[]{:S(2)}) %all-to-all-start.4) | async-done | bytes 393248 | tf_op jit(solution)/shard_map/all_to_all | solution.py:199
  173.4 4.0 %all-to-all-start.3 = ((bf16[32,128,256]{2,0,1:T(8,128)(2,1)}), bf16[32,128,256]{2,0,1:T(8,128)(2,1)S(1)}, u32[]{:S(2)}, u32[]{:S(2)}) async-start(bf16[32,128,256]{2,0,1:T(8,128)(2,1)} %copy.71), calls=%async_computation.3 | async-start | bytes 4194304 | tf_op jit(solution)/shard_map/all_to_all | solution.py:39
  178.2 40.6 %all-gather.5.cloned.1.call-done.uh_ref = bf16[16384,256]{1,0:T(8,128)(2,1)} async-done(((bf16[128,256]{1,0:T(8,128)(2,1)}), bf16[16384,256]{1,0:T(8,128)(2,1)}) %all-gather.5.cloned.1.call-update) | async-done | bytes 8388624 | tf_op jit(solution)/shard_map/all_gather | solution.py:169
  218.8 9.9 %shard_map.147 = f32[128,256]{1,0:T(8,128)} custom-call(s32[1]{0:T(128)} %bitcast.21.base_ref, f32[1]{0:T(128)} %copy.82.scale_ref, bf16[128,256]{1,0:T(8,128)(2,1)} %multiply_convert_fusion.vh_ref, bf16[16384,256]{1,0:T(8,128)(2,1)} %all-gather.5.cloned.1.call-done.uh_ref, f32[1,16384]{1,0:T(1,128)} %bitcast.86, f32[1,16384]{1,0:T(1,128)} %bitcast.85), custom_call_target="tpu_custom_call" | custom-call | tf_op jit(solution)/shard_map/pallas_call | solution.py:81
  228.7 1.1 multiply_reduce_fusion
  229.8 1.3 fusion.44
  231.2 1.3 convolution_convert_fusion
  232.8 1.2 pad_maximum_fusion.1
  234.0 6.0 %all-to-all-start.5 = ((bf16[6,128,256]{2,0,1:T(8,128)(2,1)}), bf16[6,128,256]{2,0,1:T(8,128)(2,1)S(1)}, u32[]{:S(2)}, u32[]{:S(2)}) async-start(bf16[6,128,256]{2,0,1:T(8,128)(2,1)} %pad_maximum_fusion.1), calls=%async_computation.5 | async-start | bytes 1048576 | tf_op jit(solution)/shard_map/all_to_all | solution.py:39
  240.0 1.2 slice_reduce_fusion
  241.3 2.5 copy.72
  243.8 10.3 %all-to-all-done.5 = bf16[6,128,256]{2,0,1:T(8,128)(2,1)S(1)} async-done(((bf16[6,128,256]{2,0,1:T(8,128)(2,1)}), bf16[6,128,256]{2,0,1:T(8,128)(2,1)S(1)}, u32[]{:S(2)}, u32[]{:S(2)}) %all-to-all-start.5) | async-done | bytes 393248 | tf_op jit(solution)/shard_map/all_to_all | solution.py:39
  254.4 0.9 broadcast_in_dim.55
  255.3 4.4 %all-to-all-start.6 = ((f32[128,4,256]{2,1,0:T(4,128)}), f32[128,4,256]{2,1,0:T(4,128)S(1)}, u32[]{:S(2)}, u32[]{:S(2)}) async-start(f32[128,4,256]{2,1,0:T(4,128)} %broadcast_in_dim.55), calls=%async_computation.6 | async-start | bytes 1048576 | tf_op jit(solution)/shard_map/all_to_all | solution.py:221
  259.7 14.9 %fusion = f32[4096,256]{1,0:T(8,128)} fusion(bf16[4096,256]{1,0:T(8,128)(2,1)} %bitcast.76, s32[4096]{0:T(1024)S(1)} %bitcast.96), kind=kOutput, calls=%fused_computation.2 | convolution fusion | flops 8606711808 | bytes 6307840 | tf_op jit(solution)/shard_map/dot_general | solution.py:35
  274.7 2.8 fusion.10
  277.7 0.9 reshape.324
  278.6 0.9 reshape.325
  (91 shorter events, 12.3 us)
Async XLA Ops:
  7.2 51.8 %copy-start = (bf16[4096,256]{1,0:T(8,128)(2,1)S(1)}, bf16[4096,256]{1,0:T(8,128)(2,1)}, u32[]{:S(2)}) copy-start(bf16[4096,256]{1,0:T(8,128)(2,1)} %param.12) | copy-start | bytes 6291460
  7.2 8.0 %copy-start.8 = (s32[2048,1]{0,1:T(1,128)S(1)}, s32[2048,1]{0,1:T(1,128)}, u32[]{:S(2)}) copy-start(s32[2048,1]{0,1:T(1,128)} %param.14) | copy-start | bytes 24580
  7.2 8.7 %copy-start.10 = (s32[128]{0:T(128)S(1)}, s32[128]{0:T(128)}, u32[]{:S(2)}) copy-start(s32[128]{0:T(128)} %param.20) | copy-start | bytes 1540
  7.2 8.7 %copy-start.9 = (s32[2048]{0:T(1024)S(1)}, s32[2048]{0:T(1024)}, u32[]{:S(2)}) copy-start(s32[2048]{0:T(1024)} %param.15) | copy-start | bytes 24580
  12.6 1.0 copy-start.4
  16.3 41.5 %copy-start.7 = (bf16[256,256]{1,0:T(8,128)(2,1)S(1)}, bf16[256,256]{1,0:T(8,128)(2,1)}, u32[]{:S(2)}) copy-start(bf16[256,256]{1,0:T(8,128)(2,1)} %param.22) | copy-start | bytes 393220
  18.5 21.2 %all-to-all-start = ((s32[34,128,1]{0,2,1:T(1,128)}), s32[34,128,1]{0,2,1:T(1,128)S(1)}, u32[]{:S(2)}, u32[]{:S(2)}) async-start(s32[34,128,1]{0,2,1:T(1,128)} %copy.63), calls=%async_computation | async-start | bytes 131072 | tf_op jit(solution)/shard_map/all_to_all | solution.py:39
  43.1 14.5 %all-to-all-start.2 = ((bf16[2,128,256]{2,0,1:T(2,128)(2,1)}), bf16[2,128,256]{2,0,1:T(2,128)(2,1)S(1)}, u32[]{:S(2)}, u32[]{:S(2)}) async-start(bf16[2,128,256]{2,0,1:T(2,128)(2,1)} %copy.68), calls=%async_computation.2 | async-start | bytes 262144 | tf_op jit(solution)/shard_map/all_to_all | solution.py:39
  47.4 88.0 %all-gather.3.cloned.1.call-start = ((), (), s32[]{:S(2)}) async-start(), calls=%async_computation.7 | async-start | bytes 8454144 | tf_op jit(solution)/shard_map/all_gather | solution.py:162
  71.2 6.7 %copy-start.11 = (bf16[64]{0:T(256)(128)(2,1)S(1)}, bf16[64]{0:T(256)(128)(2,1)}, u32[]{:S(2)}) copy-start(bf16[64]{0:T(256)(128)(2,1)} %param.18) | copy-start | bytes 388
  73.7 35.6 %all-to-all-start.1 = ((bf16[32,128,256]{2,0,1:T(8,128)(2,1)}), bf16[32,128,256]{2,0,1:T(8,128)(2,1)S(1)}, u32[]{:S(2)}, u32[]{:S(2)}) async-start(bf16[32,128,256]{2,0,1:T(8,128)(2,1)} %copy.65), calls=%async_computation.1 | async-start | bytes 4194304 | tf_op jit(solution)/shard_map/all_to_all | solution.py:39
  77.7 141.1 %all-gather.5.cloned.1.call-start = ((), (), s32[]{:S(2)}) async-start(), calls=%async_computation.8 | async-start | bytes 8454144 | tf_op jit(solution)/shard_map/all_gather | solution.py:169
  78.8 32.4 %copy-start.6 = (bf16[256,256]{1,0:T(8,128)(2,1)S(1)}, bf16[256,256]{1,0:T(8,128)(2,1)}, u32[]{:S(2)}) copy-start(bf16[256,256]{1,0:T(8,128)(2,1)} %param.21) | copy-start | bytes 393220
  141.7 3.4 %copy-start.3 = (bf16[16384,256]{1,0:T(8,128)(2,1)S(1)}, bf16[16384,256]{1,0:T(8,128)(2,1)}, u32[]{:S(2)}) copy-start(bf16[16384,256]{1,0:T(8,128)(2,1)} %all-gather.3.cloned.1.call-done) | copy-start | bytes 25165828
  150.3 2.0 copy-start.2
  154.0 19.4 %all-to-all-start.4 = ((f32[128,3,256]{2,1,0:T(4,128)}), f32[128,3,256]{2,1,0:T(4,128)S(1)}, u32[]{:S(2)}, u32[]{:S(2)}) async-start(f32[128,3,256]{2,1,0:T(4,128)} %pad_maximum_fusion), calls=%async_computation.4 | async-start | bytes 1048576 | tf_op jit(solution)/shard_map/all_to_all | solution.py:199
  173.4 55.3 %copy-start.5 = (f32[128,3,256]{2,1,0:T(4,128)}, f32[128,3,256]{2,1,0:T(4,128)S(1)}, u32[]{:S(2)}) copy-start(f32[128,3,256]{2,1,0:T(4,128)S(1)} %all-to-all-done.4) | copy-start | bytes 1179652
  173.4 60.6 %all-to-all-start.3 = ((bf16[32,128,256]{2,0,1:T(8,128)(2,1)}), bf16[32,128,256]{2,0,1:T(8,128)(2,1)S(1)}, u32[]{:S(2)}, u32[]{:S(2)}) async-start(bf16[32,128,256]{2,0,1:T(8,128)(2,1)} %copy.71), calls=%async_computation.3 | async-start | bytes 4194304 | tf_op jit(solution)/shard_map/all_to_all | solution.py:39
  234.0 20.1 %all-to-all-start.5 = ((bf16[6,128,256]{2,0,1:T(8,128)(2,1)}), bf16[6,128,256]{2,0,1:T(8,128)(2,1)S(1)}, u32[]{:S(2)}, u32[]{:S(2)}) async-start(bf16[6,128,256]{2,0,1:T(8,128)(2,1)} %pad_maximum_fusion.1), calls=%async_computation.5 | async-start | bytes 1048576 | tf_op jit(solution)/shard_map/all_to_all | solution.py:39
  255.3 22.2 %all-to-all-start.6 = ((f32[128,4,256]{2,1,0:T(4,128)}), f32[128,4,256]{2,1,0:T(4,128)S(1)}, u32[]{:S(2)}, u32[]{:S(2)}) async-start(f32[128,4,256]{2,1,0:T(4,128)} %broadcast_in_dim.55), calls=%async_computation.6 | async-start | bytes 1048576 | tf_op jit(solution)/shard_map/all_to_all | solution.py:221
  274.7 4.8 %copy-start.1 = (bf16[4096,256]{1,0:T(8,128)(2,1)S(1)}, bf16[4096,256]{1,0:T(8,128)(2,1)}, u32[]{:S(2)}) copy-start(bf16[4096,256]{1,0:T(8,128)(2,1)} %param.12) | copy-start | bytes 6291460
Sparse Core Ops, SparseCore 0:
  59.0 76.3 all-gather.2
  139.1 79.6 all-gather.4

commit v4 on v3

--- a/solution.py
+++ b/solution.py
@@ -51,7 +51,7 @@
     s = scale_ref[0] * lax.dot_general(
         vh_ref[...], uh, (((1,), (1,)), ((), ())), preferred_element_type=jnp.float32
     )
-    p = jnp.exp(s - top_ref[...]) / norm_ref[...]
+    p = jnp.exp(s - top_ref[...]) * (1.0 / norm_ref[...])
     col = b * block + lax.broadcasted_iota(jnp.int32, (rows, block), 1)
     mine = base_ref[0] + lax.broadcasted_iota(jnp.int32, (rows, block), 0)
     pw = (p - (col == mine).astype(jnp.float32)).astype(jnp.bfloat16)

time: 292 us -> 292 us (level)
  no operation moved by 1% of the time
where the time goes in v4:
time: 292 us; the launch traced here: 287 us
  waiting for transfers between devices  130 us (45%)
  matrix products  49.3 us (17%)
  starting transfers between devices  40.3 us (14%)
  local copies, waits for them, and re-layouts  22.4 us (8%)
  other arithmetic  19 us (7%)
  between operations  15.5 us (5%)
  Pallas kernels  9.89 us (3%)
    all_to_all x5, waiting for transfers between devices, exchange(): return lax.all_to_all(x, AXES, split_axis=1, concat_axis=1, tiled=True)  59.9 us
    all_gather x1, waiting for transfers between devices, local(): uh_all = lax.all_gather(uh, AXES, axis=0, tiled=True)  40.6 us
    all_to_all x5, starting transfers between devices, exchange(): return lax.all_to_all(x, AXES, split_axis=1, concat_axis=1, tiled=True)  29.8 us
    all_gather x1, waiting for transfers between devices, local(): vh_all = lax.all_gather(vh, AXES, axis=0, tiled=True)  22.3 us
    dot_general x2, matrix products, add_rows(): jnp.dot(onehot, values.reshape(flat.shape[0], -1), preferred_element_type...  17.7 us
    dot_general x2, matrix products, pick_rows(): jnp.dot(onehot, table, preferred_element_type=jnp.float32)  14.7 us
    pallas_call x1, Pallas kernels, column_side(): pl.pallas_call(_column_kernel, out_shape=jax.ShapeDtypeStruct((rows, widt...  9.89 us
    all_to_all x1, waiting for transfers between devices, local(): lax.all_to_all(jnp.concatenate([stats, user_parts], axis=1), AXES, split_...  7.29 us
  transfers between devices with their start and end apart: 9, of which 7 were waited for; matrix products, arithmetic and copies ran while one was open for 24% of the time, Pallas kernels for 3%

profile of v4, /device:TPU:1, one launch (start us, length us, event | category | flops | bytes accessed | tf_op | source)
XLA Modules:
  0.0 286.6 jit_solution(15349482975454919244)
XLA Ops:
  7.2 0.9 fusion.36
  10.6 0.8 select_reduce_fusion.1
  11.4 0.8 copy.61
  12.6 1.0 copy-done.4
  13.6 1.3 broadcast_add_fusion
  16.3 1.2 convolution_convert_fusion.1
  17.7 0.7 copy.63
  18.5 11.5 %all-to-all-start = ((s32[34,128,1]{0,2,1:T(1,128)}), s32[34,128,1]{0,2,1:T(1,128)S(1)}, u32[]{:S(2)}, u32[]{:S(2)}) async-start(s32[34,128,1]{0,2,1:T(1,128)} %copy.63), calls=%async_computation | async-start | bytes 131072 | tf_op jit(solution)/shard_map/all_to_all | solution.py:39
  30.0 9.7 %all-to-all-done = s32[34,128,1]{0,2,1:T(1,128)S(1)} async-done(((s32[34,128,1]{0,2,1:T(1,128)}), s32[34,128,1]{0,2,1:T(1,128)S(1)}, u32[]{:S(2)}, u32[]{:S(2)}) %all-to-all-start) | async-done | bytes 17440 | tf_op jit(solution)/shard_map/all_to_all | solution.py:39
  39.9 2.4 fusion.17
  42.3 0.8 copy.68
  43.1 4.3 %all-to-all-start.2 = ((bf16[2,128,256]{2,0,1:T(2,128)(2,1)}), bf16[2,128,256]{2,0,1:T(2,128)(2,1)S(1)}, u32[]{:S(2)}, u32[]{:S(2)}) async-start(bf16[2,128,256]{2,0,1:T(2,128)(2,1)} %copy.68), calls=%async_computation.2 | async-start | bytes 262144 | tf_op jit(solution)/shard_map/all_to_all | solution.py:39
  48.4 9.3 %all-to-all-done.2 = bf16[2,128,256]{2,0,1:T(2,128)(2,1)S(1)} async-done(((bf16[2,128,256]{2,0,1:T(2,128)(2,1)}), bf16[2,128,256]{2,0,1:T(2,128)(2,1)S(1)}, u32[]{:S(2)}, u32[]{:S(2)}) %all-to-all-start.2) | async-done | bytes 131104 | tf_op jit(solution)/shard_map/all_to_all | solution.py:39
  58.1 0.7 multiply_convert_fusion.vh_ref
  58.9 12.3 %fusion.5 = bf16[4096,256]{1,0:T(8,128)(2,1)S(1)} fusion(bf16[4096,256]{1,0:T(8,128)(2,1)S(1)} %copy-done, s32[4096]{0:T(1024)S(1)} %bitcast.95), kind=kOutput, calls=%fused_computation.11 | convolution fusion | flops 8607760384 | bytes 4210688 | tf_op jit(solution)/shard_map/dot_general | solution.py:28
  71.2 2.5 copy.65
  73.7 4.0 %all-to-all-start.1 = ((bf16[32,128,256]{2,0,1:T(8,128)(2,1)}), bf16[32,128,256]{2,0,1:T(8,128)(2,1)S(1)}, u32[]{:S(2)}, u32[]{:S(2)}) async-start(bf16[32,128,256]{2,0,1:T(8,128)(2,1)} %copy.65), calls=%async_computation.1 | async-start | bytes 4194304 | tf_op jit(solution)/shard_map/all_to_all | solution.py:39
  78.8 30.6 %all-to-all-done.1 = bf16[32,128,256]{2,0,1:T(8,128)(2,1)S(1)} async-done(((bf16[32,128,256]{2,0,1:T(8,128)(2,1)}), bf16[32,128,256]{2,0,1:T(8,128)(2,1)S(1)}, u32[]{:S(2)}, u32[]{:S(2)}) %all-to-all-start.1) | async-done | bytes 2097184 | tf_op jit(solution)/shard_map/all_to_all | solution.py:39
  109.4 1.2 copy.66
  113.1 22.3 %all-gather.3.cloned.1.call-done = bf16[16384,256]{1,0:T(8,128)(2,1)} async-done(((bf16[128,256]{1,0:T(8,128)(2,1)}), bf16[16384,256]{1,0:T(8,128)(2,1)}) %all-gather.3.cloned.1.call-update) | async-done | bytes 8388624 | tf_op jit(solution)/shard_map/all_gather | solution.py:162
  135.4 6.3 %fusion.47 = (f32[128]{0:T(128)S(1)}, f32[128,16384]{1,0:T(8,128)S(1)}) fusion(bf16[128,256]{1,0:T(8,128)(2,1)} %multiply_convert_fusion.1, bf16[16384,256]{1,0:T(8,128)(2,1)} %all-gather.3.cloned.1.call-done, f32[]{:T(128)} %bitcast.73), kind=kOutput, calls=%fused_computation.112 | convolution fusion | flops 1077936000 | bytes 16843268 | tf_op jit(solution)/shard_map/dot_general | solution.py:174
  141.7 1.6 fusion.4
  143.3 1.8 copy-done.3
  145.1 2.9 %multiply_reduce_fusion.1 = (f32[128]{0:T(128)S(1)}, f32[128,256]{1,0:T(8,128)S(1)}) fusion(f32[128,256]{1,0:T(8,128)S(1)} %get-tuple-element.21, f32[128]{0:T(128)S(1)} %add_rsqrt_fusion.1, bf16[16384,256]{1,0:T(8,128)(2,1)S(1)} %copy-done.3, f32[128,16384]{1,0:T(8,128)S(1)} %get-tuple-element.23, s32[128]{0:T(128)S(1)} %iota_add_fusion, ...), kind=kOutput, calls=%fused_computation.70 | convolution fusion | flops 1086455680 | bytes 17041924 | tf_op jit(solution)/shard_map/dot_general | solution.py:181
  148.3 2.0 fusion.15
  150.3 2.0 copy-done.2
  152.9 1.0 pad_maximum_fusion
  154.0 5.4 %all-to-all-start.4 = ((f32[128,3,256]{2,1,0:T(4,128)}), f32[128,3,256]{2,1,0:T(4,128)S(1)}, u32[]{:S(2)}, u32[]{:S(2)}) async-start(f32[128,3,256]{2,1,0:T(4,128)} %pad_maximum_fusion), calls=%async_computation.4 | async-start | bytes 1048576 | tf_op jit(solution)/shard_map/all_to_all | solution.py:199
  159.4 2.8 fusion.12
  162.7 3.4 %copy.71 = bf16[32,128,256]{2,0,1:T(8,128)(2,1)} copy(bf16[32,128,256]{1,0,2:T(8,128)(2,1)S(1)} %bitcast.75) | data formatting | bytes 4194304 | tf_op jit(solution)/shard_map/reshape | solution.py:191
  166.1 7.3 %all-to-all-done.4 = f32[128,3,256]{2,1,0:T(4,128)S(1)} async-done(((f32[128,3,256]{2,1,0:T(4,128)}), f32[128,3,256]{2,1,0:T(4,128)S(1)}, u32[]{:S(2)}, u32[]{:S(2)}) %all-to-all-start.4) | async-done | bytes 393248 | tf_op jit(solution)/shard_map/all_to_all | solution.py:199
  173.4 4.0 %all-to-all-start.3 = ((bf16[32,128,256]{2,0,1:T(8,128)(2,1)}), bf16[32,128,256]{2,0,1:T(8,128)(2,1)S(1)}, u32[]{:S(2)}, u32[]{:S(2)}) async-start(bf16[32,128,256]{2,0,1:T(8,128)(2,1)} %copy.71), calls=%async_computation.3 | async-start | bytes 4194304 | tf_op jit(solution)/shard_map/all_to_all | solution.py:39
  178.2 40.6 %all-gather.5.cloned.1.call-done.uh_ref = bf16[16384,256]{1,0:T(8,128)(2,1)} async-done(((bf16[128,256]{1,0:T(8,128)(2,1)}), bf16[16384,256]{1,0:T(8,128)(2,1)}) %all-gather.5.cloned.1.call-update) | async-done | bytes 8388624 | tf_op jit(solution)/shard_map/all_gather | solution.py:169
  218.8 9.9 %shard_map.147 = f32[128,256]{1,0:T(8,128)} custom-call(s32[1]{0:T(128)} %bitcast.21.base_ref, f32[1]{0:T(128)} %copy.82.scale_ref, bf16[128,256]{1,0:T(8,128)(2,1)} %multiply_convert_fusion.vh_ref, bf16[16384,256]{1,0:T(8,128)(2,1)} %all-gather.5.cloned.1.call-done.uh_ref, f32[1,16384]{1,0:T(1,128)} %bitcast.86, f32[1,16384]{1,0:T(1,128)} %bitcast.85), custom_call_target="tpu_custom_call" | custom-call | tf_op jit(solution)/shard_map/pallas_call | solution.py:81
  228.7 1.1 multiply_reduce_fusion
  229.8 1.3 fusion.44
  231.2 1.3 convolution_convert_fusion
  232.8 1.2 pad_maximum_fusion.1
  234.0 6.0 %all-to-all-start.5 = ((bf16[6,128,256]{2,0,1:T(8,128)(2,1)}), bf16[6,128,256]{2,0,1:T(8,128)(2,1)S(1)}, u32[]{:S(2)}, u32[]{:S(2)}) async-start(bf16[6,128,256]{2,0,1:T(8,128)(2,1)} %pad_maximum_fusion.1), calls=%async_computation.5 | async-start | bytes 1048576 | tf_op jit(solution)/shard_map/all_to_all | solution.py:39
  240.0 1.2 slice_reduce_fusion
  241.3 2.5 copy.72
  243.8 10.3 %all-to-all-done.5 = bf16[6,128,256]{2,0,1:T(8,128)(2,1)S(1)} async-done(((bf16[6,128,256]{2,0,1:T(8,128)(2,1)}), bf16[6,128,256]{2,0,1:T(8,128)(2,1)S(1)}, u32[]{:S(2)}, u32[]{:S(2)}) %all-to-all-start.5) | async-done | bytes 393248 | tf_op jit(solution)/shard_map/all_to_all | solution.py:39
  254.5 0.9 broadcast_in_dim.55
  255.3 4.4 %all-to-all-start.6 = ((f32[128,4,256]{2,1,0:T(4,128)}), f32[128,4,256]{2,1,0:T(4,128)S(1)}, u32[]{:S(2)}, u32[]{:S(2)}) async-start(f32[128,4,256]{2,1,0:T(4,128)} %broadcast_in_dim.55), calls=%async_computation.6 | async-start | bytes 1048576 | tf_op jit(solution)/shard_map/all_to_all | solution.py:221
  259.7 14.9 %fusion = f32[4096,256]{1,0:T(8,128)} fusion(bf16[4096,256]{1,0:T(8,128)(2,1)} %bitcast.76, s32[4096]{0:T(1024)S(1)} %bitcast.96), kind=kOutput, calls=%fused_computation.2 | convolution fusion | flops 8606711808 | bytes 6307840 | tf_op jit(solution)/shard_map/dot_general | solution.py:35
  274.7 2.8 fusion.10
  277.7 0.9 reshape.324
  278.6 0.9 reshape.325
  (91 shorter events, 12.3 us)
Async XLA Ops:
  7.2 51.8 %copy-start = (bf16[4096,256]{1,0:T(8,128)(2,1)S(1)}, bf16[4096,256]{1,0:T(8,128)(2,1)}, u32[]{:S(2)}) copy-start(bf16[4096,256]{1,0:T(8,128)(2,1)} %param.12) | copy-start | bytes 6291460
  7.2 8.0 %copy-start.8 = (s32[2048,1]{0,1:T(1,128)S(1)}, s32[2048,1]{0,1:T(1,128)}, u32[]{:S(2)}) copy-start(s32[2048,1]{0,1:T(1,128)} %param.14) | copy-start | bytes 24580
  7.2 8.7 %copy-start.10 = (s32[128]{0:T(128)S(1)}, s32[128]{0:T(128)}, u32[]{:S(2)}) copy-start(s32[128]{0:T(128)} %param.20) | copy-start | bytes 1540
  7.2 8.7 %copy-start.9 = (s32[2048]{0:T(1024)S(1)}, s32[2048]{0:T(1024)}, u32[]{:S(2)}) copy-start(s32[2048]{0:T(1024)} %param.15) | copy-start | bytes 24580
  12.6 1.0 copy-start.4
  16.3 41.5 %copy-start.7 = (bf16[256,256]{1,0:T(8,128)(2,1)S(1)}, bf16[256,256]{1,0:T(8,128)(2,1)}, u32[]{:S(2)}) copy-start(bf16[256,256]{1,0:T(8,128)(2,1)} %param.22) | copy-start | bytes 393220
  18.5 21.2 %all-to-all-start = ((s32[34,128,1]{0,2,1:T(1,128)}), s32[34,128,1]{0,2,1:T(1,128)S(1)}, u32[]{:S(2)}, u32[]{:S(2)}) async-start(s32[34,128,1]{0,2,1:T(1,128)} %copy.63), calls=%async_computation | async-start | bytes 131072 | tf_op jit(solution)/shard_map/all_to_all | solution.py:39
  43.1 14.5 %all-to-all-start.2 = ((bf16[2,128,256]{2,0,1:T(2,128)(2,1)}), bf16[2,128,256]{2,0,1:T(2,128)(2,1)S(1)}, u32[]{:S(2)}, u32[]{:S(2)}) async-start(bf16[2,128,256]{2,0,1:T(2,128)(2,1)} %copy.68), calls=%async_computation.2 | async-start | bytes 262144 | tf_op jit(solution)/shard_map/all_to_all | solution.py:39
  47.4 88.0 %all-gather.3.cloned.1.call-start = ((), (), s32[]{:S(2)}) async-start(), calls=%async_computation.7 | async-start | bytes 8454144 | tf_op jit(solution)/shard_map/all_gather | solution.py:162
  71.2 6.7 %copy-start.11 = (bf16[64]{0:T(256)(128)(2,1)S(1)}, bf16[64]{0:T(256)(128)(2,1)}, u32[]{:S(2)}) copy-start(bf16[64]{0:T(256)(128)(2,1)} %param.18) | copy-start | bytes 388
  73.7 35.6 %all-to-all-start.1 = ((bf16[32,128,256]{2,0,1:T(8,128)(2,1)}), bf16[32,128,256]{2,0,1:T(8,128)(2,1)S(1)}, u32[]{:S(2)}, u32[]{:S(2)}) async-start(bf16[32,128,256]{2,0,1:T(8,128)(2,1)} %copy.65), calls=%async_computation.1 | async-start | bytes 4194304 | tf_op jit(solution)/shard_map/all_to_all | solution.py:39
  77.7 141.1 %all-gather.5.cloned.1.call-start = ((), (), s32[]{:S(2)}) async-start(), calls=%async_computation.8 | async-start | bytes 8454144 | tf_op jit(solution)/shard_map/all_gather | solution.py:169
  78.8 32.4 %copy-start.6 = (bf16[256,256]{1,0:T(8,128)(2,1)S(1)}, bf16[256,256]{1,0:T(8,128)(2,1)}, u32[]{:S(2)}) copy-start(bf16[256,256]{1,0:T(8,128)(2,1)} %param.21) | copy-start | bytes 393220
  141.7 3.4 %copy-start.3 = (bf16[16384,256]{1,0:T(8,128)(2,1)S(1)}, bf16[16384,256]{1,0:T(8,128)(2,1)}, u32[]{:S(2)}) copy-start(bf16[16384,256]{1,0:T(8,128)(2,1)} %all-gather.3.cloned.1.call-done) | copy-start | bytes 25165828
  150.3 2.0 copy-start.2
  154.0 19.4 %all-to-all-start.4 = ((f32[128,3,256]{2,1,0:T(4,128)}), f32[128,3,256]{2,1,0:T(4,128)S(1)}, u32[]{:S(2)}, u32[]{:S(2)}) async-start(f32[128,3,256]{2,1,0:T(4,128)} %pad_maximum_fusion), calls=%async_computation.4 | async-start | bytes 1048576 | tf_op jit(solution)/shard_map/all_to_all | solution.py:199
  173.4 55.3 %copy-start.5 = (f32[128,3,256]{2,1,0:T(4,128)}, f32[128,3,256]{2,1,0:T(4,128)S(1)}, u32[]{:S(2)}) copy-start(f32[128,3,256]{2,1,0:T(4,128)S(1)} %all-to-all-done.4) | copy-start | bytes 1179652
  173.4 60.6 %all-to-all-start.3 = ((bf16[32,128,256]{2,0,1:T(8,128)(2,1)}), bf16[32,128,256]{2,0,1:T(8,128)(2,1)S(1)}, u32[]{:S(2)}, u32[]{:S(2)}) async-start(bf16[32,128,256]{2,0,1:T(8,128)(2,1)} %copy.71), calls=%async_computation.3 | async-start | bytes 4194304 | tf_op jit(solution)/shard_map/all_to_all | solution.py:39
  234.0 20.1 %all-to-all-start.5 = ((bf16[6,128,256]{2,0,1:T(8,128)(2,1)}), bf16[6,128,256]{2,0,1:T(8,128)(2,1)S(1)}, u32[]{:S(2)}, u32[]{:S(2)}) async-start(bf16[6,128,256]{2,0,1:T(8,128)(2,1)} %pad_maximum_fusion.1), calls=%async_computation.5 | async-start | bytes 1048576 | tf_op jit(solution)/shard_map/all_to_all | solution.py:39
  255.3 22.2 %all-to-all-start.6 = ((f32[128,4,256]{2,1,0:T(4,128)}), f32[128,4,256]{2,1,0:T(4,128)S(1)}, u32[]{:S(2)}, u32[]{:S(2)}) async-start(f32[128,4,256]{2,1,0:T(4,128)} %broadcast_in_dim.55), calls=%async_computation.6 | async-start | bytes 1048576 | tf_op jit(solution)/shard_map/all_to_all | solution.py:221
  274.7 4.8 %copy-start.1 = (bf16[4096,256]{1,0:T(8,128)(2,1)S(1)}, bf16[4096,256]{1,0:T(8,128)(2,1)}, u32[]{:S(2)}) copy-start(bf16[4096,256]{1,0:T(8,128)(2,1)} %param.12) | copy-start | bytes 6291460
Sparse Core Ops, SparseCore 0:
  59.0 76.3 all-gather.2
  139.1 79.6 all-gather.4

commit v5 on v1

--- a/solution.py
+++ b/solution.py
@@ -154,6 +154,7 @@
     top_all = flat_stats[:, :samples].reshape(total)
     norm_all = flat_stats[:, samples : 2 * samples].reshape(total)
     user_red = jnp.sum(got_s[:, n_stat:], 0)
+    uh_all, user_grad = lax.optimization_barrier((uh_all, user_grad))
     scores_c = scale * jnp.dot(vh, uh_all.T, preferred_element_type=jnp.float32)
     prob_c = jnp.exp(scores_c - top_all[None, :]) / norm_all[None, :]
     hot_c = (everyone[None, :] == mine[:, None]).astype(jnp.float32)

time: 289 us -> 289 us (level)
  blocking collectives: 0 us -> 21.1 us
  starting transfers between devices: 40.3 us -> 27.9 us
  other arithmetic: 18 us -> 12.6 us
  local copies, waits for them, and re-layouts: 22.4 us -> 17.9 us
  waiting for transfers between devices: 130 us -> 133 us
    all_gather x1, waiting for transfers between devices: 40.6 us -> 8.31 us  [local(): uh_all = lax.all_gather(uh, AXES, axis=0, tiled=True)]
    all_to_all x5 -> x4, waiting for transfers between devices: 59.9 us -> 84.1 us  [exchange(): return lax.all_to_all(x, AXES, split_axis=1, concat_axis=1, tiled=True)]
    all_to_all x0 -> x1, blocking collectives: none -> 21.1 us  [exchange(): return lax.all_to_all(x, AXES, split_axis=1, concat_axis=1, tiled=True)]
    all_to_all x5 -> x4, starting transfers between devices: 29.8 us -> 18 us  [exchange(): return lax.all_to_all(x, AXES, split_axis=1, concat_axis=1, tiled=True)]
    all_to_all x1, waiting for transfers between devices: 0.01 us -> 11.3 us  [local(): lax.all_to_all(jnp.broadcast_to(red[None], (devices,) + red.shape), AXES,...]
  transfers between devices with their start and end apart: 9 -> 8, of which waited for: 7 -> 8; matrix products, arithmetic and copies ran while one was open for 26% -> 20% of each run, Pallas kernels for 0% -> 0%
where the time goes in v5:
time: 289 us; the launch traced here: 284 us
  waiting for transfers between devices  133 us (46%)
  matrix products  55.7 us (19%)
  starting transfers between devices  27.9 us (10%)
  blocking collectives  21.1 us (7%)
  local copies, waits for them, and re-layouts  17.9 us (6%)
  between operations  15.8 us (5%)
  other arithmetic  12.6 us (4%)
    all_to_all x4, waiting for transfers between devices, exchange(): return lax.all_to_all(x, AXES, split_axis=1, concat_axis=1, tiled=True)  84.1 us
    all_gather x1, waiting for transfers between devices, local(): vh_all = lax.all_gather(vh, AXES, axis=0, tiled=True)  22.3 us
    all_to_all x1, blocking collectives, exchange(): return lax.all_to_all(x, AXES, split_axis=1, concat_axis=1, tiled=True)  21.1 us
    all_to_all x4, starting transfers between devices, exchange(): return lax.all_to_all(x, AXES, split_axis=1, concat_axis=1, tiled=True)  18 us
    dot_general x2, matrix products, add_rows(): jnp.dot(onehot, values.reshape(flat.shape[0], -1), preferred_element_type...  16 us
    dot_general x2, matrix products, pick_rows(): jnp.dot(onehot, table, preferred_element_type=jnp.float32)  14.7 us
    all_to_all x1, waiting for transfers between devices, local(): lax.all_to_all(jnp.broadcast_to(red[None], (devices,) + red.shape), AXES,...  11.3 us
    dot_general x1, matrix products, local(): jnp.dot(pw_c, uh_all, preferred_element_type=jnp.float32)  9.87 us
  transfers between devices with their start and end apart: 8, of which 8 were waited for; matrix products, arithmetic and copies ran while one was open for 20% of the time, Pallas kernels for 0%

profile of v5, /device:TPU:1, one launch (start us, length us, event | category | flops | bytes accessed | tf_op | source)
XLA Modules:
  0.0 284.2 jit_solution(5296484607041070425)
XLA Ops:
  7.3 0.9 fusion.47
  8.3 0.8 select_reduce_fusion.1
  9.2 0.8 copy.59
  10.3 1.0 copy-done.3
  11.3 1.3 broadcast_add_fusion
  13.0 0.6 fusion.33
  14.3 1.2 convolution_convert_fusion.1
  15.9 21.1 %all_to_all.36 = s32[34,128,1]{0,2,1:T(1,128)S(1)} all-to-all(s32[34,128,1]{0,2,1:T(1,128)S(1)} %copy.61), channel_id=1, replica_groups=mesh['dp'=8,'table'=16] {'dp','table'}, dimensions={1} | all-to-all | bytes 34816 | tf_op jit(solution)/shard_map/all_to_all | solution.py:37
  37.2 2.4 fusion.25
  39.6 0.8 copy.66
  40.4 4.3 %all-to-all-start.2 = ((bf16[2,128,256]{2,0,1:T(2,128)(2,1)}), bf16[2,128,256]{2,0,1:T(2,128)(2,1)S(1)}, u32[]{:S(2)}, u32[]{:S(2)}) async-start(bf16[2,128,256]{2,0,1:T(2,128)(2,1)} %copy.66), calls=%async_computation.2 | async-start | bytes 262144 | tf_op jit(solution)/shard_map/all_to_all | solution.py:37
  45.3 9.6 %all-to-all-done.2 = bf16[2,128,256]{2,0,1:T(2,128)(2,1)S(1)} async-done(((bf16[2,128,256]{2,0,1:T(2,128)(2,1)}), bf16[2,128,256]{2,0,1:T(2,128)(2,1)S(1)}, u32[]{:S(2)}, u32[]{:S(2)}) %all-to-all-start.2) | async-done | bytes 131104 | tf_op jit(solution)/shard_map/all_to_all | solution.py:37
  55.4 0.7 multiply_convert_fusion
  56.2 12.3 %fusion.11 = bf16[4096,256]{1,0:T(8,128)(2,1)S(1)} fusion(bf16[4096,256]{1,0:T(8,128)(2,1)S(1)} %copy-done, s32[4096]{0:T(1024)S(1)} %bitcast.99), kind=kOutput, calls=%fused_computation.18 | convolution fusion | flops 8607760384 | bytes 4210688 | tf_op jit(solution)/shard_map/dot_general | solution.py:26
  68.5 2.5 copy.63
  71.0 4.0 %all-to-all-start.1 = ((bf16[32,128,256]{2,0,1:T(8,128)(2,1)}), bf16[32,128,256]{2,0,1:T(8,128)(2,1)S(1)}, u32[]{:S(2)}, u32[]{:S(2)}) async-start(bf16[32,128,256]{2,0,1:T(8,128)(2,1)} %copy.63), calls=%async_computation.1 | async-start | bytes 4194304 | tf_op jit(solution)/shard_map/all_to_all | solution.py:37
  75.6 0.5 convert_reduce_fusion
  76.1 30.6 %all-to-all-done.1 = bf16[32,128,256]{2,0,1:T(8,128)(2,1)S(1)} async-done(((bf16[32,128,256]{2,0,1:T(8,128)(2,1)}), bf16[32,128,256]{2,0,1:T(8,128)(2,1)S(1)}, u32[]{:S(2)}, u32[]{:S(2)}) %all-to-all-start.1) | async-done | bytes 2097184 | tf_op jit(solution)/shard_map/all_to_all | solution.py:37
  106.7 1.2 copy.64
  107.8 0.7 fusion.30
  108.8 0.7 multiply_convert_fusion.1
  110.4 22.3 %all-gather.5.cloned.1.call-done = bf16[16384,256]{1,0:T(8,128)(2,1)} async-done(((bf16[128,256]{1,0:T(8,128)(2,1)}), bf16[16384,256]{1,0:T(8,128)(2,1)}) %all-gather.5.cloned.1.call-update) | async-done | bytes 8388624 | tf_op jit(solution)/shard_map/all_gather | solution.py:113
  132.7 6.3 %fusion.58 = (f32[128]{0:T(128)S(1)}, f32[128,16384]{1,0:T(8,128)S(1)}) fusion(bf16[128,256]{1,0:T(8,128)(2,1)} %multiply_convert_fusion.1, bf16[16384,256]{1,0:T(8,128)(2,1)} %all-gather.5.cloned.1.call-done, f32[]{:T(128)} %bitcast.77), kind=kOutput, calls=%fused_computation.123 | convolution fusion | flops 1077936000 | bytes 16843268 | tf_op jit(solution)/shard_map/dot_general | solution.py:125
  139.0 1.6 fusion.10
  140.6 1.8 copy-done.2
  142.4 2.9 %multiply_reduce_fusion.1 = (f32[128]{0:T(128)S(1)}, f32[128,256]{1,0:T(8,128)S(1)}) fusion(f32[128,256]{1,0:T(8,128)S(1)} %get-tuple-element.22, f32[128]{0:T(128)S(1)} %add_rsqrt_fusion.1, bf16[16384,256]{1,0:T(8,128)(2,1)S(1)} %copy-done.2, f32[128,16384]{1,0:T(8,128)S(1)} %get-tuple-element.26, s32[128]{0:T(128)S(1)} %iota_add_fusion, ...), kind=kOutput, calls=%fused_computation.79 | convolution fusion | flops 1086455680 | bytes 17041924 | tf_op jit(solution)/shard_map/dot_general | solution.py:132
  145.9 1.0 pad_maximum_fusion
  147.0 5.4 %all-to-all-start.4 = ((f32[128,3,256]{2,1,0:T(4,128)}), f32[128,3,256]{2,1,0:T(4,128)S(1)}, u32[]{:S(2)}, u32[]{:S(2)}) async-start(f32[128,3,256]{2,1,0:T(4,128)} %pad_maximum_fusion), calls=%async_computation.4 | async-start | bytes 1048576 | tf_op jit(solution)/shard_map/all_to_all | solution.py:150
  152.7 1.9 fusion.23
  154.6 0.6 fusion.19
  155.3 0.5 copy.76
  155.7 3.4 %copy.69 = bf16[32,128,256]{2,0,1:T(8,128)(2,1)} copy(bf16[32,128,256]{1,0,2:T(8,128)(2,1)S(1)} %bitcast.80) | data formatting | bytes 4194304 | tf_op jit(solution)/shard_map/reshape | solution.py:142
  159.2 7.2 %all-to-all-done.4 = f32[128,3,256]{2,1,0:T(4,128)S(1)} async-done(((f32[128,3,256]{2,1,0:T(4,128)}), f32[128,3,256]{2,1,0:T(4,128)S(1)}, u32[]{:S(2)}, u32[]{:S(2)}) %all-to-all-start.4) | async-done | bytes 393248 | tf_op jit(solution)/shard_map/all_to_all | solution.py:150
  166.4 4.4 %all-to-all-start.3 = ((bf16[32,128,256]{2,0,1:T(8,128)(2,1)}), bf16[32,128,256]{2,0,1:T(8,128)(2,1)S(1)}, u32[]{:S(2)}, u32[]{:S(2)}) async-start(bf16[32,128,256]{2,0,1:T(8,128)(2,1)} %copy.69), calls=%async_computation.3 | async-start | bytes 4194304 | tf_op jit(solution)/shard_map/all_to_all | solution.py:37
  170.9 30.1 %all-to-all-done.3 = bf16[32,128,256]{2,0,1:T(8,128)(2,1)S(1)} async-done(((bf16[32,128,256]{2,0,1:T(8,128)(2,1)}), bf16[32,128,256]{2,0,1:T(8,128)(2,1)S(1)}, u32[]{:S(2)}, u32[]{:S(2)}) %all-to-all-start.3) | async-done | bytes 2097184 | tf_op jit(solution)/shard_map/all_to_all | solution.py:37
  201.0 1.2 copy.70
  202.2 13.3 %fusion.1 = f32[4096,256]{1,0:T(8,128)} fusion(bf16[4096,256]{1,0:T(8,128)(2,1)S(1)} %bitcast.82, s32[4096]{0:T(1024)S(1)} %bitcast.100), kind=kOutput, calls=%fused_computation.3 | convolution fusion | flops 8606711808 | bytes 6307840 | tf_op jit(solution)/shard_map/dot_general | solution.py:33
  215.5 8.3 %all-gather.3.cloned.1.call-done = bf16[16384,256]{1,0:T(8,128)(2,1)} async-done(((bf16[128,256]{1,0:T(8,128)(2,1)}), bf16[16384,256]{1,0:T(8,128)(2,1)}) %all-gather.3.cloned.1.call-update) | async-done | bytes 8388624 | tf_op jit(solution)/shard_map/all_gather | solution.py:120
  223.8 9.9 %multiply_reduce_fusion = (f32[128]{0:T(128)S(1)}, f32[128,256]{1,0:T(8,128)S(1)}) fusion(f32[128,256]{1,0:T(8,128)S(1)} %get-tuple-element.24, f32[128]{0:T(128)S(1)} %add_rsqrt_fusion, bf16[16384,256]{1,0:T(8,128)(2,1)} %all-gather.3.cloned.1.call-done, bf16[128,256]{1,0:T(8,128)(2,1)S(1)} %copy-done.5, f32[16384]{0:T(1024)S(1)} %get-tuple-element.18, ...), kind=kOutput, calls=%fused_computation.77 | convolution fusion | flops 2162294784 | bytes 8848904 | tf_op jit(solution)/shard_map/dot_general | solution.py:162
  234.9 1.2 pad_maximum_fusion.1
  236.1 5.4 %all-to-all-start.5 = ((bf16[6,128,256]{2,0,1:T(8,128)(2,1)}), bf16[6,128,256]{2,0,1:T(8,128)(2,1)S(1)}, u32[]{:S(2)}, u32[]{:S(2)}) async-start(bf16[6,128,256]{2,0,1:T(8,128)(2,1)} %pad_maximum_fusion.1), calls=%async_computation.5 | async-start | bytes 1048576 | tf_op jit(solution)/shard_map/all_to_all | solution.py:37
  241.7 13.8 %all-to-all-done.5 = bf16[6,128,256]{2,0,1:T(8,128)(2,1)S(1)} async-done(((bf16[6,128,256]{2,0,1:T(8,128)(2,1)}), bf16[6,128,256]{2,0,1:T(8,128)(2,1)S(1)}, u32[]{:S(2)}, u32[]{:S(2)}) %all-to-all-start.5) | async-done | bytes 393248 | tf_op jit(solution)/shard_map/all_to_all | solution.py:37
  255.9 0.9 broadcast_in_dim.55
  256.7 4.0 %all-to-all-start.6 = ((f32[128,4,256]{2,1,0:T(4,128)}), f32[128,4,256]{2,1,0:T(4,128)S(1)}, u32[]{:S(2)}, u32[]{:S(2)}) async-start(f32[128,4,256]{2,1,0:T(4,128)} %broadcast_in_dim.55), calls=%async_computation.6 | async-start | bytes 1048576 | tf_op jit(solution)/shard_map/all_to_all | solution.py:177
  260.9 2.8 fusion.17
  263.7 11.3 %all-to-all-done.6 = f32[128,4,256]{2,1,0:T(4,128)S(1)} async-done(((f32[128,4,256]{2,1,0:T(4,128)}), f32[128,4,256]{2,1,0:T(4,128)S(1)}, u32[]{:S(2)}, u32[]{:S(2)}) %all-to-all-start.6) | async-done | bytes 524320 | tf_op jit(solution)/shard_map/all_to_all | solution.py:177
  275.2 0.9 reshape.322
  276.0 0.9 reshape.323
  (93 shorter events, 7.3 us)
Async XLA Ops:
  7.2 49.0 %copy-start = (bf16[4096,256]{1,0:T(8,128)(2,1)S(1)}, bf16[4096,256]{1,0:T(8,128)(2,1)}, u32[]{:S(2)}) copy-start(bf16[4096,256]{1,0:T(8,128)(2,1)} %param.12) | copy-start | bytes 6291460
  7.2 5.8 %copy-start.11 = (s32[128,1]{0,1:T(1,128)S(1)}, s32[128,1]{0,1:T(1,128)}, u32[]{:S(2)}) copy-start(s32[128,1]{0,1:T(1,128)} %param.19) | copy-start | bytes 1540
  7.2 5.8 %copy-start.7 = (s32[2048,1]{0,1:T(1,128)S(1)}, s32[2048,1]{0,1:T(1,128)}, u32[]{:S(2)}) copy-start(s32[2048,1]{0,1:T(1,128)} %param.14) | copy-start | bytes 24580
  7.2 6.5 %copy-start.9 = (s32[1,2048]{1,0:T(1,128)S(1)}, s32[1,2048]{1,0:T(1,128)}, u32[]{:S(2)}) copy-start(s32[1,2048]{1,0:T(1,128)} %param.16) | copy-start | bytes 24580
  7.2 6.6 %copy-start.10 = (s32[2048]{0:T(1024)S(1)}, s32[2048]{0:T(1024)}, u32[]{:S(2)}) copy-start(s32[2048]{0:T(1024)} %param.17) | copy-start | bytes 24580
  7.2 6.6 %copy-start.8 = (s32[2048]{0:T(1024)S(1)}, s32[2048]{0:T(1024)}, u32[]{:S(2)}) copy-start(s32[2048]{0:T(1024)} %param.15) | copy-start | bytes 24580
  7.2 6.6 %copy-start.12 = (s32[128]{0:T(128)S(1)}, s32[128]{0:T(128)}, u32[]{:S(2)}) copy-start(s32[128]{0:T(128)} %param.20) | copy-start | bytes 1540
  10.3 1.0 copy-start.3
  14.3 40.8 %copy-start.6 = (bf16[256,256]{1,0:T(8,128)(2,1)S(1)}, bf16[256,256]{1,0:T(8,128)(2,1)}, u32[]{:S(2)}) copy-start(bf16[256,256]{1,0:T(8,128)(2,1)} %param.22) | copy-start | bytes 393220
  40.4 14.5 %all-to-all-start.2 = ((bf16[2,128,256]{2,0,1:T(2,128)(2,1)}), bf16[2,128,256]{2,0,1:T(2,128)(2,1)S(1)}, u32[]{:S(2)}, u32[]{:S(2)}) async-start(bf16[2,128,256]{2,0,1:T(2,128)(2,1)} %copy.66), calls=%async_computation.2 | async-start | bytes 262144 | tf_op jit(solution)/shard_map/all_to_all | solution.py:37
  44.7 88.0 %all-gather.5.cloned.1.call-start = ((), (), s32[]{:S(2)}) async-start(), calls=%async_computation.8 | async-start | bytes 8454144 | tf_op jit(solution)/shard_map/all_gather | solution.py:113
  68.5 6.8 %copy-start.13 = (bf16[64]{0:T(256)(128)(2,1)S(1)}, bf16[64]{0:T(256)(128)(2,1)}, u32[]{:S(2)}) copy-start(bf16[64]{0:T(256)(128)(2,1)} %param.18) | copy-start | bytes 388
  71.0 35.6 %all-to-all-start.1 = ((bf16[32,128,256]{2,0,1:T(8,128)(2,1)}), bf16[32,128,256]{2,0,1:T(8,128)(2,1)S(1)}, u32[]{:S(2)}, u32[]{:S(2)}) async-start(bf16[32,128,256]{2,0,1:T(8,128)(2,1)} %copy.63), calls=%async_computation.1 | async-start | bytes 4194304 | tf_op jit(solution)/shard_map/all_to_all | solution.py:37
  75.0 148.8 %all-gather.3.cloned.1.call-start = ((), (), s32[]{:S(2)}) async-start(), calls=%async_computation.7 | async-start | bytes 8454144 | tf_op jit(solution)/shard_map/all_gather | solution.py:120
  76.1 32.4 %copy-start.4 = (bf16[256,256]{1,0:T(8,128)(2,1)S(1)}, bf16[256,256]{1,0:T(8,128)(2,1)}, u32[]{:S(2)}) copy-start(bf16[256,256]{1,0:T(8,128)(2,1)} %param.21) | copy-start | bytes 393220
  139.0 3.4 %copy-start.2 = (bf16[16384,256]{1,0:T(8,128)(2,1)S(1)}, bf16[16384,256]{1,0:T(8,128)(2,1)}, u32[]{:S(2)}) copy-start(bf16[16384,256]{1,0:T(8,128)(2,1)} %all-gather.5.cloned.1.call-done) | copy-start | bytes 25165828
  147.0 19.4 %all-to-all-start.4 = ((f32[128,3,256]{2,1,0:T(4,128)}), f32[128,3,256]{2,1,0:T(4,128)S(1)}, u32[]{:S(2)}, u32[]{:S(2)}) async-start(f32[128,3,256]{2,1,0:T(4,128)} %pad_maximum_fusion), calls=%async_computation.4 | async-start | bytes 1048576 | tf_op jit(solution)/shard_map/all_to_all | solution.py:150
  166.4 34.6 %all-to-all-start.3 = ((bf16[32,128,256]{2,0,1:T(8,128)(2,1)}), bf16[32,128,256]{2,0,1:T(8,128)(2,1)S(1)}, u32[]{:S(2)}, u32[]{:S(2)}) async-start(bf16[32,128,256]{2,0,1:T(8,128)(2,1)} %copy.69), calls=%async_computation.3 | async-start | bytes 4194304 | tf_op jit(solution)/shard_map/all_to_all | solution.py:37
  202.2 21.6 %copy-start.5 = (bf16[128,256]{1,0:T(8,128)(2,1)S(1)}, bf16[128,256]{1,0:T(8,128)(2,1)}, u32[]{:S(2)}) copy-start(bf16[128,256]{1,0:T(8,128)(2,1)} %multiply_convert_fusion) | copy-start | bytes 196612
  236.1 19.4 %all-to-all-start.5 = ((bf16[6,128,256]{2,0,1:T(8,128)(2,1)}), bf16[6,128,256]{2,0,1:T(8,128)(2,1)S(1)}, u32[]{:S(2)}, u32[]{:S(2)}) async-start(bf16[6,128,256]{2,0,1:T(8,128)(2,1)} %pad_maximum_fusion.1), calls=%async_computation.5 | async-start | bytes 1048576 | tf_op jit(solution)/shard_map/all_to_all | solution.py:37
  256.7 18.2 %all-to-all-start.6 = ((f32[128,4,256]{2,1,0:T(4,128)}), f32[128,4,256]{2,1,0:T(4,128)S(1)}, u32[]{:S(2)}, u32[]{:S(2)}) async-start(f32[128,4,256]{2,1,0:T(4,128)} %broadcast_in_dim.55), calls=%async_computation.6 | async-start | bytes 1048576 | tf_op jit(solution)/shard_map/all_to_all | solution.py:177
  260.9 16.0 %copy-start.1 = (bf16[4096,256]{1,0:T(8,128)(2,1)S(1)}, bf16[4096,256]{1,0:T(8,128)(2,1)}, u32[]{:S(2)}) copy-start(bf16[4096,256]{1,0:T(8,128)(2,1)} %param.12) | copy-start | bytes 6291460
Sparse Core Ops, SparseCore 0:
  56.3 76.3 all-gather.4
  136.4 87.3 all-gather.2

commit v6 on v1

--- a/solution.py
+++ b/solution.py
@@ -139,8 +139,6 @@
     per_slot = jnp.dot(of_sample[:, :n_user].T.astype(jnp.float32), pick, precision=highest)
     g_slot = (wts[:n_user].astype(jnp.float32) / per_slot[:, width])[:, None] * per_slot[:, :width]
     g_slot = jnp.where(filled[:n_user, None], g_slot, 0.0)
-    got_user = exchange(g_slot.astype(jnp.bfloat16).reshape(cap, devices, width))
-    user_grad = add_rows(rows_dev, user_want, got_user)
     stats = jnp.concatenate([top, norm]).reshape(1, 1, -1)
     stats = jnp.broadcast_to(stats, (devices, 1, stats.shape[-1]))
     stats = jnp.pad(stats, ((0, 0), (0, 0), (0, -stats.shape[-1] % width)))
@@ -154,6 +152,26 @@
     top_all = flat_stats[:, :samples].reshape(total)
     norm_all = flat_stats[:, samples : 2 * samples].reshape(total)
     user_red = jnp.sum(got_s[:, n_stat:], 0)
+    pieces = []
+    rest = user_red
+    for _ in range(3):
+        piece = rest.astype(jnp.bfloat16)
+        pieces.append(piece)
+        rest = rest - piece.astype(jnp.float32)
+    pieces = jnp.concatenate(pieces)
+    n_piece = pieces.shape[0]
+    got_user = exchange(
+        jnp.concatenate(
+            [
+                g_slot.astype(jnp.bfloat16).reshape(cap, devices, width),
+                jnp.broadcast_to(pieces[:, None], (n_piece, devices, width)),
+            ]
+        )
+    )
+    chunk_u = user_red.shape[0]
+    spread_u = got_user[cap:].astype(jnp.float32).reshape(3, chunk_u, devices, width).sum(0)
+    user_proj_grad = jnp.transpose(spread_u, (1, 0, 2)).reshape(width, width)
+    user_grad = add_rows(rows_dev, user_want, got_user[:cap])
     scores_c = scale * jnp.dot(vh, uh_all.T, preferred_element_type=jnp.float32)
     prob_c = jnp.exp(scores_c - top_all[None, :]) / norm_all[None, :]
     hot_c = (everyone[None, :] == mine[:, None]).astype(jnp.float32)
@@ -172,12 +190,10 @@
     got = exchange(send)
     tail = got[cap_item:].astype(jnp.float32)
     goods_red = jnp.sum(tail[:chunk] + tail[chunk:], 1)
-    red = jnp.concatenate([user_red, goods_red])
     spread = lax.all_to_all(
-        jnp.broadcast_to(red[None], (devices,) + red.shape), AXES, split_axis=0, concat_axis=0, tiled=True
-    )
-    user_proj_grad = spread[:, :chunk].reshape(width, width)
-    item_proj_grad = spread[:, chunk:].reshape(width, width)
+        jnp.broadcast_to(goods_red[None], (devices,) + goods_red.shape), AXES, split_axis=0, concat_axis=0, tiled=True
+    )
+    item_proj_grad = spread.reshape(width, width)
     item_grad = add_rows(rows_dev, goods_want, got[:cap_item])
     return (user_grad, item_grad, user_proj_grad, item_proj_grad)
 

time: 289 us -> 327 us (1.13)
  waiting for transfers between devices: 130 us -> 156 us
  blocking collectives: 0 us -> 21.1 us
  starting transfers between devices: 40.3 us -> 30 us
    all_to_all x0 -> x1, blocking collectives: none -> 21.1 us  [exchange(): return lax.all_to_all(x, AXES, split_axis=1, concat_axis=1, tiled=True)]
    all_to_all x5 -> x4, waiting for transfers between devices: 59.9 us -> 75.7 us  [exchange(): return lax.all_to_all(x, AXES, split_axis=1, concat_axis=1, tiled=True)]
    all_to_all x5 -> x4, starting transfers between devices: 29.8 us -> 19 us  [exchange(): return lax.all_to_all(x, AXES, split_axis=1, concat_axis=1, tiled=True)]
    all_to_all x1, waiting for transfers between devices: 0.01 us -> 9.58 us  [local(): lax.all_to_all(jnp.broadcast_to(goods_red[None], (devices,) + goods_red.s...]
  transfers between devices with their start and end apart: 9 -> 8, of which waited for: 7 -> 8; matrix products, arithmetic and copies ran while one was open for 26% -> 15% of each run, Pallas kernels for 0% -> 0%
where the time goes in v6:
time: 327 us; the launch traced here: 322 us
  waiting for transfers between devices  156 us (48%)
  matrix products  55.8 us (17%)
  starting transfers between devices  30 us (9%)
  local copies, waits for them, and re-layouts  23.6 us (7%)
  blocking collectives  21.1 us (6%)
  other arithmetic  19.4 us (6%)
  between operations  15.6 us (5%)
    all_to_all x4, waiting for transfers between devices, exchange(): return lax.all_to_all(x, AXES, split_axis=1, concat_axis=1, tiled=True)  75.7 us
    all_gather x1, waiting for transfers between devices, local(): uh_all = lax.all_gather(uh, AXES, axis=0, tiled=True)  39.2 us
    all_gather x1, waiting for transfers between devices, local(): vh_all = lax.all_gather(vh, AXES, axis=0, tiled=True)  22.3 us
    all_to_all x1, blocking collectives, exchange(): return lax.all_to_all(x, AXES, split_axis=1, concat_axis=1, tiled=True)  21.1 us
    all_to_all x4, starting transfers between devices, exchange(): return lax.all_to_all(x, AXES, split_axis=1, concat_axis=1, tiled=True)  19 us
    dot_general x2, matrix products, add_rows(): jnp.dot(onehot, values.reshape(flat.shape[0], -1), preferred_element_type...  16 us
    dot_general x2, matrix products, pick_rows(): jnp.dot(onehot, table, preferred_element_type=jnp.float32)  14.7 us
    dot_general x1, matrix products, local(): jnp.dot(pw_c, uh_all, preferred_element_type=jnp.float32)  9.87 us
  transfers between devices with their start and end apart: 8, of which 8 were waited for; matrix products, arithmetic and copies ran while one was open for 15% of the time, Pallas kernels for 0%

profile of v6, /device:TPU:1, one launch (start us, length us, event | category | flops | bytes accessed | tf_op | source)
XLA Modules:
  0.0 321.7 jit_solution(10901684266013534306)
XLA Ops:
  7.2 0.9 fusion.47
  8.8 0.9 fusion.31
  11.4 0.8 select_reduce_fusion.1
  12.2 0.8 copy.65
  14.6 1.3 broadcast_multiply_fusion
  16.0 1.2 convolution_convert_fusion.1
  17.6 21.1 %all_to_all.36 = s32[34,128,1]{0,2,1:T(1,128)S(1)} all-to-all(s32[34,128,1]{0,2,1:T(1,128)S(1)} %copy.67), channel_id=1, replica_groups=mesh['dp'=8,'table'=16] {'dp','table'}, dimensions={1} | all-to-all | bytes 34816 | tf_op jit(solution)/shard_map/all_to_all | solution.py:37
  38.9 2.4 fusion.25
  41.3 0.8 copy.72
  42.1 4.3 %all-to-all-start.2 = ((bf16[2,128,256]{2,0,1:T(2,128)(2,1)}), bf16[2,128,256]{2,0,1:T(2,128)(2,1)S(1)}, u32[]{:S(2)}, u32[]{:S(2)}) async-start(bf16[2,128,256]{2,0,1:T(2,128)(2,1)} %copy.72), calls=%async_computation.2 | async-start | bytes 262144 | tf_op jit(solution)/shard_map/all_to_all | solution.py:37
  47.3 9.3 %all-to-all-done.2 = bf16[2,128,256]{2,0,1:T(2,128)(2,1)S(1)} async-done(((bf16[2,128,256]{2,0,1:T(2,128)(2,1)}), bf16[2,128,256]{2,0,1:T(2,128)(2,1)S(1)}, u32[]{:S(2)}, u32[]{:S(2)}) %all-to-all-start.2) | async-done | bytes 131104 | tf_op jit(solution)/shard_map/all_to_all | solution.py:37
  57.1 0.7 multiply_convert_fusion
  57.9 12.3 %fusion.11 = bf16[4096,256]{1,0:T(8,128)(2,1)S(1)} fusion(bf16[4096,256]{1,0:T(8,128)(2,1)S(1)} %copy-done, s32[4096]{0:T(1024)S(1)} %bitcast.104), kind=kOutput, calls=%fused_computation.18 | convolution fusion | flops 8607760384 | bytes 4210688 | tf_op jit(solution)/shard_map/dot_general | solution.py:26
  70.2 2.5 copy.69
  72.7 4.0 %all-to-all-start.1 = ((bf16[32,128,256]{2,0,1:T(8,128)(2,1)}), bf16[32,128,256]{2,0,1:T(8,128)(2,1)S(1)}, u32[]{:S(2)}, u32[]{:S(2)}) async-start(bf16[32,128,256]{2,0,1:T(8,128)(2,1)} %copy.69), calls=%async_computation.1 | async-start | bytes 4194304 | tf_op jit(solution)/shard_map/all_to_all | solution.py:37
  77.7 30.6 %all-to-all-done.1 = bf16[32,128,256]{2,0,1:T(8,128)(2,1)S(1)} async-done(((bf16[32,128,256]{2,0,1:T(8,128)(2,1)}), bf16[32,128,256]{2,0,1:T(8,128)(2,1)S(1)}, u32[]{:S(2)}, u32[]{:S(2)}) %all-to-all-start.1) | async-done | bytes 2097184 | tf_op jit(solution)/shard_map/all_to_all | solution.py:37
  108.3 1.2 copy.70
  112.0 22.3 %all-gather.3.cloned.1.call-done = bf16[16384,256]{1,0:T(8,128)(2,1)} async-done(((bf16[128,256]{1,0:T(8,128)(2,1)}), bf16[16384,256]{1,0:T(8,128)(2,1)}) %all-gather.3.cloned.1.call-update) | async-done | bytes 8388624 | tf_op jit(solution)/shard_map/all_gather | solution.py:113
  134.3 6.3 %fusion.59 = (f32[128]{0:T(128)S(1)}, f32[128,16384]{1,0:T(8,128)S(1)}) fusion(bf16[128,256]{1,0:T(8,128)(2,1)} %multiply_convert_fusion.1, bf16[16384,256]{1,0:T(8,128)(2,1)} %all-gather.3.cloned.1.call-done, f32[]{:T(128)} %bitcast.80), kind=kOutput, calls=%fused_computation.128 | convolution fusion | flops 1077936000 | bytes 16843268 | tf_op jit(solution)/shard_map/dot_general | solution.py:125
  140.7 1.6 fusion.10
  142.2 1.8 copy-done.3
  144.1 2.9 multiply_reduce_fusion.1
  147.6 1.0 pad_maximum_fusion.1
  148.6 5.7 %all-to-all-start.3 = ((f32[128,3,256]{2,1,0:T(4,128)}), f32[128,3,256]{2,1,0:T(4,128)S(1)}, u32[]{:S(2)}, u32[]{:S(2)}) async-start(f32[128,3,256]{2,1,0:T(4,128)} %pad_maximum_fusion.1), calls=%async_computation.3 | async-start | bytes 1048576 | tf_op jit(solution)/shard_map/all_to_all | solution.py:148
  154.7 2.0 fusion.23
  156.6 2.0 copy-done.2
  158.7 9.6 %all-to-all-done.3 = f32[128,3,256]{2,1,0:T(4,128)S(1)} async-done(((f32[128,3,256]{2,1,0:T(4,128)}), f32[128,3,256]{2,1,0:T(4,128)S(1)}, u32[]{:S(2)}, u32[]{:S(2)}) %all-to-all-start.3) | async-done | bytes 393248 | tf_op jit(solution)/shard_map/all_to_all | solution.py:148
  168.4 39.2 %all-gather.5.cloned.1.call-done = bf16[16384,256]{1,0:T(8,128)(2,1)} async-done(((bf16[128,256]{1,0:T(8,128)(2,1)}), bf16[16384,256]{1,0:T(8,128)(2,1)}) %all-gather.5.cloned.1.call-update) | async-done | bytes 8388624 | tf_op jit(solution)/shard_map/all_gather | solution.py:120
  207.6 9.9 %multiply_reduce_fusion = (f32[128]{0:T(128)S(1)}, f32[128,256]{1,0:T(8,128)S(1)}) fusion(f32[128,256]{1,0:T(8,128)S(1)} %get-tuple-element.19, f32[128]{0:T(128)S(1)} %add_rsqrt_fusion, bf16[16384,256]{1,0:T(8,128)(2,1)} %all-gather.5.cloned.1.call-done, bf16[128,256]{1,0:T(8,128)(2,1)S(1)} %copy-done.5, f32[16384]{0:T(1024)S(1)} %get-tuple-element.12, ...), kind=kOutput, calls=%fused_computation.79 | convolution fusion | flops 2162294784 | bytes 8848904 | tf_op jit(solution)/shard_map/dot_general | solution.py:179
  218.7 1.2 pad_maximum_fusion.2
  219.9 5.4 %all-to-all-start.5 = ((bf16[6,128,256]{2,0,1:T(8,128)(2,1)}), bf16[6,128,256]{2,0,1:T(8,128)(2,1)S(1)}, u32[]{:S(2)}, u32[]{:S(2)}) async-start(bf16[6,128,256]{2,0,1:T(8,128)(2,1)} %pad_maximum_fusion.2), calls=%async_computation.5 | async-start | bytes 1048576 | tf_op jit(solution)/shard_map/all_to_all | solution.py:37
  225.3 2.8 fusion.19
  228.1 1.8 copy.86
  229.9 3.9 %copy.75 = bf16[32,128,256]{2,0,1:T(8,128)(2,1)S(1)} copy(bf16[32,128,256]{1,0,2:T(8,128)(2,1)} %bitcast.83) | data formatting | bytes 4194304 | tf_op jit(solution)/shard_map/reshape | solution.py:166
  234.0 5.3 %all-to-all-done.5 = bf16[6,128,256]{2,0,1:T(8,128)(2,1)S(1)} async-done(((bf16[6,128,256]{2,0,1:T(8,128)(2,1)}), bf16[6,128,256]{2,0,1:T(8,128)(2,1)S(1)}, u32[]{:S(2)}, u32[]{:S(2)}) %all-to-all-start.5) | async-done | bytes 393248 | tf_op jit(solution)/shard_map/all_to_all | solution.py:37
  239.7 0.8 broadcast_in_dim.58
  240.5 4.5 %all-to-all-start.6 = ((f32[128,2,256]{2,1,0:T(2,128)}), f32[128,2,256]{2,1,0:T(2,128)S(1)}, u32[]{:S(2)}, u32[]{:S(2)}) async-start(f32[128,2,256]{2,1,0:T(2,128)} %broadcast_in_dim.58), calls=%async_computation.6 | async-start | bytes 524288 | tf_op jit(solution)/shard_map/all_to_all | solution.py:193
  245.0 1.8 pad_maximum_fusion
  246.8 9.6 %all-to-all-done.6 = f32[128,2,256]{2,1,0:T(2,128)S(1)} async-done(((f32[128,2,256]{2,1,0:T(2,128)}), f32[128,2,256]{2,1,0:T(2,128)S(1)}, u32[]{:S(2)}, u32[]{:S(2)}) %all-to-all-start.6) | async-done | bytes 262176 | tf_op jit(solution)/shard_map/all_to_all | solution.py:193
  256.4 5.4 %all-to-all-start.4 = ((bf16[38,128,256]{2,0,1:T(8,128)(2,1)}), bf16[38,128,256]{2,0,1:T(8,128)(2,1)}, u32[]{:S(2)}, u32[]{:S(2)}) async-start(bf16[38,128,256]{2,0,1:T(8,128)(2,1)} %pad_maximum_fusion), calls=%async_computation.4 | async-start | bytes 5242880 | tf_op jit(solution)/shard_map/all_to_all | solution.py:37
  261.9 2.8 fusion.17
  264.7 0.9 reshape.332
  265.6 30.5 %all-to-all-done.4 = bf16[38,128,256]{2,0,1:T(8,128)(2,1)} async-done(((bf16[38,128,256]{2,0,1:T(8,128)(2,1)}), bf16[38,128,256]{2,0,1:T(8,128)(2,1)}, u32[]{:S(2)}, u32[]{:S(2)}) %all-to-all-start.4) | async-done | bytes 2490400 | tf_op jit(solution)/shard_map/all_to_all | solution.py:37
  296.1 1.8 slice.129
  297.9 1.2 copy.83
  299.1 13.3 %fusion = f32[4096,256]{1,0:T(8,128)} fusion(bf16[4096,256]{1,0:T(8,128)(2,1)S(1)} %bitcast.85, s32[4096]{0:T(1024)S(1)} %bitcast.105), kind=kOutput, calls=%fused_computation.2 | convolution fusion | flops 8606711808 | bytes 6307840 | tf_op jit(solution)/shard_map/dot_general | solution.py:33
  312.3 1.1 slice.134
  313.7 0.9 reshape.331
  (94 shorter events, 12.1 us)
Async XLA Ops:
  7.2 50.7 %copy-start = (bf16[4096,256]{1,0:T(8,128)(2,1)S(1)}, bf16[4096,256]{1,0:T(8,128)(2,1)}, u32[]{:S(2)}) copy-start(bf16[4096,256]{1,0:T(8,128)(2,1)} %param.12) | copy-start | bytes 6291460
  7.2 6.7 %copy-start.7 = (s32[2048,1]{0,1:T(1,128)S(1)}, s32[2048,1]{0,1:T(1,128)}, u32[]{:S(2)}) copy-start(s32[2048,1]{0,1:T(1,128)} %param.14) | copy-start | bytes 24580
  7.2 7.3 %copy-start.9 = (s32[128]{0:T(128)S(1)}, s32[128]{0:T(128)}, u32[]{:S(2)}) copy-start(s32[128]{0:T(128)} %param.20) | copy-start | bytes 1540
  7.2 7.3 %copy-start.8 = (s32[2048]{0:T(1024)S(1)}, s32[2048]{0:T(1024)}, u32[]{:S(2)}) copy-start(s32[2048]{0:T(1024)} %param.15) | copy-start | bytes 24580
  16.0 40.8 %copy-start.6 = (bf16[256,256]{1,0:T(8,128)(2,1)S(1)}, bf16[256,256]{1,0:T(8,128)(2,1)}, u32[]{:S(2)}) copy-start(bf16[256,256]{1,0:T(8,128)(2,1)} %param.22) | copy-start | bytes 393220
  42.1 14.5 %all-to-all-start.2 = ((bf16[2,128,256]{2,0,1:T(2,128)(2,1)}), bf16[2,128,256]{2,0,1:T(2,128)(2,1)S(1)}, u32[]{:S(2)}, u32[]{:S(2)}) async-start(bf16[2,128,256]{2,0,1:T(2,128)(2,1)} %copy.72), calls=%async_computation.2 | async-start | bytes 262144 | tf_op jit(solution)/shard_map/all_to_all | solution.py:37
  46.4 88.0 %all-gather.3.cloned.1.call-start = ((), (), s32[]{:S(2)}) async-start(), calls=%async_computation.7 | async-start | bytes 8454144 | tf_op jit(solution)/shard_map/all_gather | solution.py:113
  70.2 6.7 %copy-start.10 = (bf16[64]{0:T(256)(128)(2,1)S(1)}, bf16[64]{0:T(256)(128)(2,1)}, u32[]{:S(2)}) copy-start(bf16[64]{0:T(256)(128)(2,1)} %param.18) | copy-start | bytes 388
  72.7 35.6 %all-to-all-start.1 = ((bf16[32,128,256]{2,0,1:T(8,128)(2,1)}), bf16[32,128,256]{2,0,1:T(8,128)(2,1)S(1)}, u32[]{:S(2)}, u32[]{:S(2)}) async-start(bf16[32,128,256]{2,0,1:T(8,128)(2,1)} %copy.69), calls=%async_computation.1 | async-start | bytes 4194304 | tf_op jit(solution)/shard_map/all_to_all | solution.py:37
  76.7 130.9 %all-gather.5.cloned.1.call-start = ((), (), s32[]{:S(2)}) async-start(), calls=%async_computation.8 | async-start | bytes 8454144 | tf_op jit(solution)/shard_map/all_gather | solution.py:120
  77.7 32.4 %copy-start.4 = (bf16[256,256]{1,0:T(8,128)(2,1)S(1)}, bf16[256,256]{1,0:T(8,128)(2,1)}, u32[]{:S(2)}) copy-start(bf16[256,256]{1,0:T(8,128)(2,1)} %param.21) | copy-start | bytes 393220
  140.7 3.4 %copy-start.3 = (bf16[16384,256]{1,0:T(8,128)(2,1)S(1)}, bf16[16384,256]{1,0:T(8,128)(2,1)}, u32[]{:S(2)}) copy-start(bf16[16384,256]{1,0:T(8,128)(2,1)} %all-gather.3.cloned.1.call-done) | copy-start | bytes 25165828
  148.6 19.6 %all-to-all-start.3 = ((f32[128,3,256]{2,1,0:T(4,128)}), f32[128,3,256]{2,1,0:T(4,128)S(1)}, u32[]{:S(2)}, u32[]{:S(2)}) async-start(f32[128,3,256]{2,1,0:T(4,128)} %pad_maximum_fusion.1), calls=%async_computation.3 | async-start | bytes 1048576 | tf_op jit(solution)/shard_map/all_to_all | solution.py:148
  154.7 53.0 %copy-start.5 = (bf16[128,256]{1,0:T(8,128)(2,1)S(1)}, bf16[128,256]{1,0:T(8,128)(2,1)}, u32[]{:S(2)}) copy-start(bf16[128,256]{1,0:T(8,128)(2,1)} %multiply_convert_fusion) | copy-start | bytes 196612
  156.6 2.0 copy-start.2
  219.9 19.4 %all-to-all-start.5 = ((bf16[6,128,256]{2,0,1:T(8,128)(2,1)}), bf16[6,128,256]{2,0,1:T(8,128)(2,1)S(1)}, u32[]{:S(2)}, u32[]{:S(2)}) async-start(bf16[6,128,256]{2,0,1:T(8,128)(2,1)} %pad_maximum_fusion.2), calls=%async_computation.5 | async-start | bytes 1048576 | tf_op jit(solution)/shard_map/all_to_all | solution.py:37
  240.5 15.9 %all-to-all-start.6 = ((f32[128,2,256]{2,1,0:T(2,128)}), f32[128,2,256]{2,1,0:T(2,128)S(1)}, u32[]{:S(2)}, u32[]{:S(2)}) async-start(f32[128,2,256]{2,1,0:T(2,128)} %broadcast_in_dim.58), calls=%async_computation.6 | async-start | bytes 524288 | tf_op jit(solution)/shard_map/all_to_all | solution.py:193
  256.4 39.7 %all-to-all-start.4 = ((bf16[38,128,256]{2,0,1:T(8,128)(2,1)}), bf16[38,128,256]{2,0,1:T(8,128)(2,1)}, u32[]{:S(2)}, u32[]{:S(2)}) async-start(bf16[38,128,256]{2,0,1:T(8,128)(2,1)} %pad_maximum_fusion), calls=%async_computation.4 | async-start | bytes 5242880 | tf_op jit(solution)/shard_map/all_to_all | solution.py:37
  299.0 15.6 %copy-start.1 = (bf16[4096,256]{1,0:T(8,128)(2,1)S(1)}, bf16[4096,256]{1,0:T(8,128)(2,1)}, u32[]{:S(2)}) copy-start(bf16[4096,256]{1,0:T(8,128)(2,1)} %param.12) | copy-start | bytes 6291460
Sparse Core Ops, SparseCore 0:
  58.0 76.3 all-gather.2
  138.0 69.5 all-gather.4
